TPU v7x, 128 devices: a whole 4x4x4 slice. The times are simulated.
128 devices in a mesh: gx: 16 (over x, y), gy: 8 (over z, core).
Axes of the slice: x: 4, y: 4, z: 4, core: 2. Of those that a mesh axis runs over, the one named last changes fastest.
Arguments:
- fields: bfloat16 [10, 32, 1024, 1024], P(None, None, 'gx', 'gy'), as said below
- dense_list: int32 [8, 16, 20], replicated, may hold values from -1 to 63, as said below
- filter_device: int32 [8, 16, 20], replicated, may hold values from -1 to 15, as said below
- pencil_order: int32 [32], replicated, may hold values from 0 to 31, each once
Outputs:
- tile_stats: float32 [1024, 2048], P(('gx', 'gy'))
- coarse_closure: float32 [32, 1024], P('gy')
Inputs may be any that keep to these rules, and one draw needn't show every extreme that they name: `dense_list`: row [gy, gx] lists distinct local tile indices of device (gx, gy), its listed entries first and -1 after them; in every gy row the busiest device lists 20 tiles and some list only a few. `filter_device`: -1 exactly where dense_list is -1; within a gy row each gx index receives exactly 8 listed tiles and at most 2 from any one listing device, and that most is met. `fields`: channel 0 lies between 0.05 and 0.6; channels 8 and 9 are positive.
All inputs are finite; a program needn't handle non-finite values.
Results may differ from a plain program's by a relative error of at most 0.0003.
Values may be sent and summed in bfloat16 or wider, within the bound.
No kernel may reach another device: no remote copies, remote signals or barrier semaphores. Data moves between devices by JAX's collectives and lax.ppermute only.
A program may use at most 192 MiB of HBM per device.

v0:
```python
import jax
import jax.numpy as jnp
from jax import lax
from jax.sharding import PartitionSpec as P

TE = 16
HW = 4
CAP = 2


HIGHEST = lax.Precision.HIGHEST


def with_halo(block, sides, width):
    for axis, dim in sides:
        count = lax.axis_size(axis)
        forward = [(i, i + 1) for i in range(count - 1)]
        forward.append((count - 1, 0))
        backward = [(target, source) for source, target in forward]
        low = lax.ppermute(
            lax.slice_in_dim(block, block.shape[dim] - width, None, axis=dim), axis, forward
        )
        high = lax.ppermute(lax.slice_in_dim(block, 0, width, axis=dim), axis, backward)
        block = jnp.concatenate([low, block, high], axis=dim)
    return block


def band_matrix(half_width):
    span = TE + 2 * HW
    row_index = lax.broadcasted_iota(jnp.int32, (TE, span), 0)
    column_index = lax.broadcasted_iota(jnp.int32, (TE, span), 1)
    inside = jnp.abs(column_index - row_index - HW) <= half_width
    return jnp.where(inside, 1.0 / (2 * half_width + 1), 0.0).astype(jnp.float32)


def plane_matrix(half_width):
    span = TE + 2 * HW
    weights = band_matrix(half_width)
    return jnp.einsum("ax,by->xyab", weights, weights, precision=HIGHEST).reshape(
        span * span, TE * TE
    )


def box_band(columns, half_width):
    along_z = jnp.einsum("az,qtzp->qtap", band_matrix(half_width), columns, precision=HIGHEST)
    return jnp.einsum("qtap,pc->qtac", along_z, plane_matrix(half_width), precision=HIGHEST)


def quantities(tiles):
    span = TE + 2 * HW
    tile_count = tiles.shape[0]
    cell_values = tiles.astype(jnp.float32).reshape(tile_count, tiles.shape[1], span, span * span)
    solid = cell_values[:, 0]
    gas_speed = [cell_values[:, 1 + direction] for direction in range(3)]
    grain_speed = [cell_values[:, 4 + direction] for direction in range(3)]
    pressure = cell_values[:, 7]
    granular = cell_values[:, 8]
    friction = cell_values[:, 9]
    quantity_list = [solid] + gas_speed + [pressure, friction]
    quantity_list = quantity_list + [solid * speed for speed in gas_speed]
    quantity_list = quantity_list + [solid * speed for speed in grain_speed]
    quantity_list = quantity_list + [solid * granular, solid * pressure]
    quantity_list = quantity_list + [
        friction * (gas_speed[direction] - grain_speed[direction]) for direction in range(3)
    ]
    return jnp.stack(quantity_list, axis=0)


def block_matrix():
    sub_edge = TE // 4
    plane_index = lax.broadcasted_iota(jnp.int32, (TE * TE, sub_edge * sub_edge), 0)
    block_index = lax.broadcasted_iota(jnp.int32, (TE * TE, sub_edge * sub_edge), 1)
    block_of = plane_index // TE // 4 * sub_edge + plane_index % TE // 4
    return jnp.where(block_of == block_index, 1.0 / 16.0, 0.0).astype(jnp.float32)


def closure_blocks(smoothed):
    solid_mean = smoothed[0]
    components = []
    for direction in range(3):
        components.append(smoothed[6 + direction] / solid_mean - smoothed[1 + direction])
    for direction in range(3):
        components.append(
            smoothed[14 + direction]
            - smoothed[5] * (smoothed[6 + direction] - smoothed[9 + direction]) / solid_mean
        )
    components.append(smoothed[12] / solid_mean)
    components.append(smoothed[13] / solid_mean - smoothed[4])
    sub_edge = TE // 4
    stacked = jnp.stack(components, axis=0)
    tile_count = stacked.shape[1]
    depth_mean = jnp.mean(stacked.reshape(8, tile_count, sub_edge, 4, TE * TE), axis=3)
    blocks = jnp.einsum("ktzp,pc->ktzc", depth_mean, block_matrix(), precision=HIGHEST)
    return blocks.reshape(8, tile_count, sub_edge**3)


def tile_statistics(tiles):
    total_tiles = tiles.shape[0]
    columns = quantities(tiles)
    results = []
    for half_width in range(1, HW + 1):
        results.append(closure_blocks(box_band(columns, half_width)))
    mapped = jnp.stack(results, axis=0)
    return jnp.transpose(mapped, (2, 0, 1, 3)).reshape(total_tiles, HW * 8 * (TE // 4) ** 3)


def cut_tiles(padded, tile_ids, across_x, across_y):
    span = TE + 2 * HW
    depth_at = tile_ids // (across_x * across_y)
    column_at = tile_ids // across_y % across_x
    row_at = tile_ids % across_y

    def single_tile(depth_one, column_one, row_one):
        return lax.dynamic_slice(
            padded,
            (jnp.int32(0), depth_one * TE, column_one * TE, row_one * TE),
            (padded.shape[0], span, span, span),
        )

    pieces = jax.vmap(single_tile)(depth_at, column_at, row_at)
    return pieces.reshape(tile_ids.shape[0], padded.shape[0], span * span * span)


def shards(fields, dense_list, filter_device, pencil_order):
    groups_x = lax.axis_size("gx")
    groups_y = lax.axis_size("gy")
    self_column = lax.axis_index("gx")
    self_row = lax.axis_index("gy")
    span = TE + 2 * HW
    across_x = fields.shape[2] // TE
    across_y = fields.shape[3] // TE
    list_length = dense_list.shape[2]
    per_filter = groups_x // 4 * (CAP + (CAP - 1) // 2)
    padded = with_halo(fields, (("gx", 2), ("gy", 3)), HW)
    padded = jnp.concatenate([padded[:, -HW:], padded, padded[:, :HW]], axis=1)
    own_tiles = dense_list[self_row, self_column]
    own_targets = filter_device[self_row, self_column]
    is_listed = own_targets >= 0
    before_mask = lax.broadcasted_iota(
        jnp.int32, (list_length, list_length), 0
    ) < lax.broadcasted_iota(jnp.int32, (list_length, list_length), 1)
    same_target = own_targets[:, None] == own_targets[None, :]
    send_rank = jnp.sum((same_target & before_mask).astype(jnp.int32), axis=0)
    send_slot = jnp.where(is_listed, own_targets * CAP + send_rank, groups_x * CAP)
    group_targets = filter_device[self_row]
    group_tiles = dense_list[self_row]
    arriving = (group_targets == self_column).astype(jnp.int32)
    row_rank = jnp.cumsum(arriving, axis=1) - arriving
    source_no = lax.broadcasted_iota(jnp.int32, (groups_x, list_length), 0)
    arrival_slot = (source_no * CAP + row_rank).reshape(-1)
    arrival_order = jnp.cumsum(arriving.reshape(-1)) - 1
    arrival_pos = jnp.where(arriving.reshape(-1) > 0, arrival_order, per_filter)
    take_slot = jnp.zeros((per_filter,), jnp.int32).at[arrival_pos].set(arrival_slot, mode="drop")
    take_tile = (
        jnp.zeros((per_filter,), jnp.int32)
        .at[arrival_pos]
        .set(group_tiles.reshape(-1), mode="drop")
    )
    take_source = (
        jnp.zeros((per_filter,), jnp.int32).at[arrival_pos].set(source_no.reshape(-1), mode="drop")
    )
    slot_tiles = jnp.zeros((groups_x * CAP,), jnp.int32).at[send_slot].set(own_tiles, mode="drop")
    outgoing = cut_tiles(padded, slot_tiles, across_x, across_y).reshape(
        groups_x, CAP, fields.shape[0], span**3
    )
    incoming = lax.all_to_all(outgoing, "gx", split_axis=0, concat_axis=0, tiled=True)
    chosen = incoming.reshape(groups_x * CAP, fields.shape[0], span**3)[take_slot]
    statistics = tile_statistics(chosen)
    tile_means = jnp.mean(
        statistics.reshape(per_filter, HW * 8, statistics.shape[1] // (HW * 8)), axis=2
    )
    tile_x = take_source * across_x + take_tile // across_y % across_x
    tile_y = self_row * across_y + take_tile % across_y
    pencils = pencil_order.shape[0]
    coarse_x = across_x * groups_x // 2
    pencil_index = lax.broadcasted_iota(jnp.int32, (per_filter, pencils), 1)
    owner_row = jnp.sum(
        jnp.where(pencil_order[None, :] == (tile_y // 2)[:, None], pencil_index, 0), axis=1
    )
    cell_no = owner_row * coarse_x + tile_x // 2
    placing = (
        lax.broadcasted_iota(jnp.int32, (pencils * coarse_x, per_filter), 0) == cell_no[None, :]
    ).astype(jnp.float32)
    partial_sums = jnp.dot(
        placing, tile_means, precision=HIGHEST, preferred_element_type=jnp.float32
    ).reshape(pencils, coarse_x * HW * 8)
    per_row = pencils // groups_y
    row_pencils = lax.dynamic_slice_in_dim(pencil_order, self_row * per_row, per_row)
    every_tile = dense_list.reshape(-1)
    every_valid = every_tile >= 0
    every_group = lax.broadcasted_iota(jnp.int32, dense_list.shape, 0).reshape(-1)
    every_source = lax.broadcasted_iota(jnp.int32, dense_list.shape, 1).reshape(-1)
    every_y = (every_group * across_y + every_tile % across_y) // 2
    every_x = (every_source * across_x + every_tile // across_y % across_x) // 2
    in_row = ((row_pencils[:, None] == every_y[None, :]) & every_valid[None, :]).astype(jnp.float32)
    in_column = (
        every_x[:, None] == lax.broadcasted_iota(jnp.int32, (every_x.shape[0], coarse_x), 1)
    ).astype(jnp.float32)
    tile_counts = jnp.dot(in_row, in_column, precision=HIGHEST, preferred_element_type=jnp.float32)
    summed = lax.psum(partial_sums, ("gx", "gy"))
    own_rows = lax.dynamic_slice_in_dim(summed, self_row * per_row, per_row, 0)
    averaged = (
        own_rows.reshape(per_row, coarse_x, HW * 8) / jnp.maximum(tile_counts, 1.0)[:, :, None]
    )
    return (statistics, averaged.reshape(per_row, coarse_x * HW * 8))


def solution(mesh):
    in_specs = (P(None, None, "gx", "gy"), P(), P(), P())
    out_specs = (P(("gx", "gy"), None), P("gy", None))
    return jax.shard_map(shards, mesh=mesh, in_specs=in_specs, out_specs=out_specs, check_vma=False)
```

profile of v0, /device:TPU:1, one launch (start us, length us, event | category | flops | bytes accessed | tf_op | source)
XLA Modules:
  0.0 903.4 jit_solution(9419652497696424480)
XLA Ops:
  16.3 15.6 %copy.111 = bf16[10,32,64,128]{2,1,3,0:T(8,128)(2,1)} copy(bf16[10,32,64,128]{3,2,1,0:T(8,128)(2,1)} %param.4) | data formatting | bytes 10485760 | tf_op args[0]
  33.1 7.8 copy.110
  41.0 7.7 copy.112
  60.1 65.8 %fusion = bf16[10,40,72,136]{2,1,3,0:T(8,128)(2,1)} fusion(bf16[10,32,72,4]{2,1,3,0:T(8,128)(2,1)S(1)} %collective-permute-done.3, bf16[10,32,72,4]{2,1,3,0:T(8,128)(2,1)S(1)} %collective-permute-done.2, bf16[10,32,4,128]{2,1,3,0:T(8,128)(2,1)S(1)} %copy-done, bf16[10,32,64,128]{2,1,3,0:T(8,128)(2,1)} %copy.111, bf16[10,32,4,128]{2,1,3,0:T(8,128)(2,1)S(1)} %bitcast.294), kind=kLoop, calls=%fused_computation.9 | loop fusion | flops 117504000 | bytes 14100480 | tf_op jit(solution)/shard_map/concatenate | solution.py:135
  125.9 239.9 %while.1 = (s32[]{:T(128)}, bf16[10,40,72,136]{2,1,3,0:T(8,128)(2,1)}, s32[32,4]{0,1:T(4,128)S(1)}, bf16[32,10,24,24,24]{4,3,2,1,0:T(8,128)(2,1)}, s32[]{:T(128)}) while((s32[]{:T(128)}, bf16[10,40,72,136]{2,1,3,0:T(8,128)(2,1)}, s32[32,4]{0,1:T(4,128)S(1)}, bf16[32,10,24,24,24]{4,3,2,1,0:T(8,128)(2,1)}, s32[]{:T(128)}) %tuple.62), condition=%wide.while_cond, body=%wide.while_body.sunk | while | flops 2 | bytes 2857605 | solution.py:114
  126.5 4.5 constant_dynamic-slice_fusion.8
  134.1 4.5 constant_dynamic-slice_fusion.8
  163.9 4.5 constant_dynamic-slice_fusion.8
  171.5 4.5 constant_dynamic-slice_fusion.8
  179.1 4.5 constant_dynamic-slice_fusion.8
  209.0 4.5 constant_dynamic-slice_fusion.8
  216.5 4.5 constant_dynamic-slice_fusion.8
  254.1 4.5 constant_dynamic-slice_fusion.8
  261.7 4.5 constant_dynamic-slice_fusion.8
  269.3 4.5 constant_dynamic-slice_fusion.8
  284.2 4.5 constant_dynamic-slice_fusion.8
  365.8 73.3 %reshape.579 = bf16[16,2,10,13824]{3,2,1,0:T(8,128)(2,1)} reshape(bf16[32,10,24,24,24]{4,3,2,1,0:T(8,128)(2,1)} %get-tuple-element.9) | data formatting | bytes 17694720 | tf_op jit(solution)/shard_map/reshape;reshape | solution.py:163
  439.1 17.2 %copy.115 = bf16[16,2,10,13824]{3,1,2,0:T(2,128)(2,1)} copy(bf16[16,2,10,13824]{3,2,1,0:T(8,128)(2,1)} %reshape.579) | data formatting | bytes 17694720 | tf_op jit(solution)/shard_map/reshape;reshape | solution.py:163
  456.3 5.0 all-to-all-start
  485.6 132.6 %all-to-all-done = bf16[16,2,10,13824]{3,1,2,0:T(2,128)(2,1)} async-done(((bf16[16,2,10,13824]{3,1,2,0:T(2,128)(2,1)}), bf16[16,2,10,13824]{3,1,2,0:T(2,128)(2,1)}, u32[]{:S(2)}, u32[]{:S(2)}) %all-to-all-start) | async-done | bytes 8847392 | tf_op jit(solution)/shard_map/all_to_all | solution.py:166
  618.1 12.8 %copy.116 = bf16[16,2,10,13824]{3,2,1,0:T(8,128)(2,1)} copy(bf16[16,2,10,13824]{3,1,2,0:T(2,128)(2,1)} %all-to-all-done) | data formatting | bytes 17694720 | tf_op jit(solution)/shard_map/all_to_all | solution.py:166
  631.0 5.9 gather_fusion
  640.3 6.3 reshape.525
  656.5 5.4 fusion.112
  661.9 6.2 fusion.8
  669.8 5.4 fusion.110
  675.2 6.3 fusion.6
  683.1 5.4 fusion.108
  688.6 6.1 fusion.4
  695.3 5.4 fusion.106
  700.7 6.1 fusion.2
  751.4 143.6 %all-reduce.3.cloned.1.call-done = f32[32,1024]{1,0:T(8,128)} async-done(((f32[32,1024]{1,0:T(8,128)}), f32[32,1024]{1,0:T(8,128)}) %all-reduce.3.cloned.1.call-update) | async-done | bytes 131088 | tf_op jit(solution)/shard_map/psum | solution.py:200
  (362 shorter events, 298.8 us)
Async XLA Ops:
  8.9 24.2 %collective-permute-start = (bf16[10,32,4,128]{3,1,2,0:T(8,128)(2,1)S(1)}, bf16[10,32,4,128]{3,1,2,0:T(8,128)(2,1)S(1)}, u32[]{:S(2)}, u32[]{:S(2)}) collective-permute-start(bf16[10,32,4,128]{3,1,2,0:T(8,128)(2,1)S(1)} %copy.157), channel_id=1, source_target_pairs={{0,8},{8,16},{16,24},{24,32},{32,40},{40,48},{48,56},{56,64},{64,7... | collective-permute-start | bytes 983048 | tf_op jit(solution)/shard_map/ppermute | solution.py:20
  11.1 29.8 %collective-permute-start.1 = (bf16[10,32,4,128]{3,1,2,0:T(8,128)(2,1)S(1)}, bf16[10,32,4,128]{3,1,2,0:T(8,128)(2,1)S(1)}, u32[]{:S(2)}, u32[]{:S(2)}) collective-permute-start(bf16[10,32,4,128]{3,1,2,0:T(8,128)(2,1)S(1)} %copy.158), channel_id=1, source_target_pairs={{8,0},{16,8},{24,16},{32,24},{40,32},{48,40},{56,48},{64,56},{72,6... | collective-permute-start | bytes 983048 | tf_op jit(solution)/shard_map/ppermute | solution.py:23
  41.0 19.1 %slice-start = ((s8[10485760]{0:T(1024)(128)(4,1)}), s8[2097152]{0:T(1024)(128)(4,1)S(1)}, s32[]{:S(2)}) async-start(s8[10485760]{0:T(1024)(128)(4,1)} %bitcast.293), calls=%async_computation.2 | async-start | bytes 4194304
  48.7 11.4 %slice-start.1 = ((s8[10485760]{0:T(1024)(128)(4,1)}), s8[4194304]{0:T(1024)(128)(4,1)S(1)}, s32[]{:S(2)}) async-start(s8[10485760]{0:T(1024)(128)(4,1)} %bitcast.293), calls=%async_computation.3 | async-start | bytes 8388608
  48.7 11.4 %slice-start.2 = ((s8[10485760]{0:T(1024)(128)(4,1)}), s8[4194304]{0:T(1024)(128)(4,1)S(1)}, s32[]{:S(2)}) async-start(s8[10485760]{0:T(1024)(128)(4,1)} %bitcast.293), calls=%async_computation.4 | async-start | bytes 8388608
  48.7 11.4 %copy-start = (bf16[10,32,4,128]{2,1,3,0:T(8,128)(2,1)S(1)}, bf16[10,32,4,128]{2,1,3,0:T(8,128)(2,1)}, u32[]{:S(2)}) copy-start(bf16[10,32,4,128]{2,1,3,0:T(8,128)(2,1)} %copy.112) | copy-start | bytes 983044
  50.9 6.6 collective-permute-start.2
  53.5 6.5 collective-permute-start.3
  456.3 5.2 copy-start.7
  456.3 161.8 %all-to-all-start = ((bf16[16,2,10,13824]{3,1,2,0:T(2,128)(2,1)}), bf16[16,2,10,13824]{3,1,2,0:T(2,128)(2,1)}, u32[]{:S(2)}, u32[]{:S(2)}) async-start(bf16[16,2,10,13824]{3,1,2,0:T(2,128)(2,1)} %copy.115), calls=%async_computation | async-start | bytes 17694720 | tf_op jit(solution)/shard_map/all_to_all | solution.py:166
  461.3 433.7 %all-reduce.3.cloned.1.call-start = ((), (), s32[]{:S(2)}) async-start(), calls=%async_computation.1 | async-start | bytes 262144 | tf_op jit(solution)/shard_map/psum | solution.py:200
  466.4 15.2 %copy-start.8 = (s32[32]{0:T(128)S(1)}, s32[32]{0:T(128)}, u32[]{:S(2)}) copy-start(s32[32]{0:T(128)} %param.7) | copy-start | bytes 388
  646.5 9.3 %copy-start.1 = (f32[8,10,24,576]{3,2,0,1:T(8,128)S(1)}, f32[8,10,24,576]{3,2,0,1:T(8,128)}, u32[]{:S(2)}) copy-start(f32[8,10,24,576]{3,2,0,1:T(8,128)} %reshape.525) | copy-start | bytes 13271044
  656.4 5.5 copy-start.5
  668.9 6.3 copy-start.4
  682.2 6.3 copy-start.3
  694.7 6.0 copy-start.2
  741.9 5.3 copy-start.6
Sparse Core Ops, SparseCore 0:
  750.0 144.9 all-reduce.2
where the time goes:
time: 910 us; the launch traced here: 903 us
  local copies, waits for them, and re-layouts  447 us (49%)
  waiting for transfers between devices  283 us (31%)
  other arithmetic  91.9 us (10%)
  matrix products  52.6 us (6%)
  between operations  15.2 us (2%)
  starting transfers between devices  13.7 us (2%)
    gather x160, local copies, waits for them, and re-layouts  239 us
    psum x1, waiting for transfers between devices, shards(): summed = lax.psum(partial_sums, ('gx', 'gy'))  144 us
    all_to_all x1, waiting for transfers between devices, shards(): lax.all_to_all(outgoing, 'gx', split_axis=0, concat_axis=0, tiled=True)  133 us
    another operation x2, local copies, waits for them, and re-layouts, shards(): cut_tiles(padded, slot_tiles, across_x, across_y)  90.5 us
    concatenate x1, other arithmetic, shards(): padded = jnp.concatenate([padded[:, -HW:], padded, padded[:, :HW]], axis=1)  65.8 us
    unnamed x61, local copies, waits for them, and re-layouts  33 us
    dot_general x4, matrix products, box_band(): jnp.einsum('qtap,pc->qtac', along_z, plane_matrix(half_width), precision=...  24.6 us
    dot_general x4, matrix products, box_band(): jnp.einsum('az,qtzp->qtap', band_matrix(half_width), columns, precision=H...  21.6 us
  transfers between devices with their start and end apart: 6, of which 4 were waited for; matrix products, arithmetic and copies ran while one was open for 6% of the time, Pallas kernels for 0%

commit v1 on v0

--- a/solution.py
+++ b/solution.py
@@ -126,7 +126,6 @@
     groups_y = lax.axis_size("gy")
     self_column = lax.axis_index("gx")
     self_row = lax.axis_index("gy")
-    span = TE + 2 * HW
     across_x = fields.shape[2] // TE
     across_y = fields.shape[3] // TE
     list_length = dense_list.shape[2]
@@ -159,33 +158,37 @@
     take_source = (
         jnp.zeros((per_filter,), jnp.int32).at[arrival_pos].set(source_no.reshape(-1), mode="drop")
     )
-    slot_tiles = jnp.zeros((groups_x * CAP,), jnp.int32).at[send_slot].set(own_tiles, mode="drop")
-    outgoing = cut_tiles(padded, slot_tiles, across_x, across_y).reshape(
-        groups_x, CAP, fields.shape[0], span**3
+    own_cut = cut_tiles(padded, jnp.where(is_listed, own_tiles, 0), across_x, across_y)
+    own_statistics = tile_statistics(own_cut)
+    stat_length = own_statistics.shape[1]
+    outgoing = (
+        jnp.zeros((groups_x * CAP, stat_length), jnp.float32)
+        .at[send_slot]
+        .set(own_statistics, mode="drop")
+        .reshape(groups_x, CAP, stat_length)
     )
     incoming = lax.all_to_all(outgoing, "gx", split_axis=0, concat_axis=0, tiled=True)
-    chosen = incoming.reshape(groups_x * CAP, fields.shape[0], span**3)[take_slot]
-    statistics = tile_statistics(chosen)
+    statistics = incoming.reshape(groups_x * CAP, stat_length)[take_slot]
     tile_means = jnp.mean(
-        statistics.reshape(per_filter, HW * 8, statistics.shape[1] // (HW * 8)), axis=2
+        statistics.reshape(per_filter, HW * 8, stat_length // (HW * 8)), axis=2
     )
     tile_x = take_source * across_x + take_tile // across_y % across_x
     tile_y = self_row * across_y + take_tile % across_y
     pencils = pencil_order.shape[0]
     coarse_x = across_x * groups_x // 2
-    pencil_index = lax.broadcasted_iota(jnp.int32, (per_filter, pencils), 1)
-    owner_row = jnp.sum(
-        jnp.where(pencil_order[None, :] == (tile_y // 2)[:, None], pencil_index, 0), axis=1
-    )
-    cell_no = owner_row * coarse_x + tile_x // 2
+    per_row = pencils // groups_y
+    local_pencil = tile_y // 2 - self_row * per_row
+    cell_no = local_pencil * coarse_x + tile_x // 2
     placing = (
-        lax.broadcasted_iota(jnp.int32, (pencils * coarse_x, per_filter), 0) == cell_no[None, :]
+        lax.broadcasted_iota(jnp.int32, (per_row * coarse_x, per_filter), 0) == cell_no[None, :]
     ).astype(jnp.float32)
     partial_sums = jnp.dot(
         placing, tile_means, precision=HIGHEST, preferred_element_type=jnp.float32
-    ).reshape(pencils, coarse_x * HW * 8)
-    per_row = pencils // groups_y
+    ).reshape(per_row, coarse_x * HW * 8)
+    row_sums = lax.psum(partial_sums, "gx")
+    all_rows = lax.all_gather(row_sums, "gy", axis=0, tiled=True)
     row_pencils = lax.dynamic_slice_in_dim(pencil_order, self_row * per_row, per_row)
+    own_rows = all_rows[row_pencils]
     every_tile = dense_list.reshape(-1)
     every_valid = every_tile >= 0
     every_group = lax.broadcasted_iota(jnp.int32, dense_list.shape, 0).reshape(-1)
@@ -197,8 +200,6 @@
         every_x[:, None] == lax.broadcasted_iota(jnp.int32, (every_x.shape[0], coarse_x), 1)
     ).astype(jnp.float32)
     tile_counts = jnp.dot(in_row, in_column, precision=HIGHEST, preferred_element_type=jnp.float32)
-    summed = lax.psum(partial_sums, ("gx", "gy"))
-    own_rows = lax.dynamic_slice_in_dim(summed, self_row * per_row, per_row, 0)
     averaged = (
         own_rows.reshape(per_row, coarse_x, HW * 8) / jnp.maximum(tile_counts, 1.0)[:, :, None]
     )

time: 910 us -> 681 us (0.75)
  waiting for transfers between devices: 283 us -> 5.6 us
  local copies, waits for them, and re-layouts: 447 us -> 322 us
  blocking collectives: 0 us -> 86.8 us
  matrix products: 52.6 us -> 134 us
  other arithmetic: 91.9 us -> 107 us
  between operations: 15.2 us -> 1.93 us
    psum x1 -> x0, waiting for transfers between devices: 144 us -> none  [shards(): summed = lax.psum(partial_sums, ('gx', 'gy'))]
    all_to_all x1, waiting for transfers between devices: 133 us -> 0.2 us  [shards(): lax.all_to_all(outgoing, 'gx', split_axis=0, concat_axis=0, tiled=True)]
    gather x161 -> x102, local copies, waits for them, and re-layouts: 245 us -> 152 us
    another operation x3 -> x2, local copies, waits for them, and re-layouts: 90.6 us -> 0.12 us  [the longest x2 90.5 us: shards(): cut_tiles(padded, slot_tiles, across_x, across_y)]
    psum x0 -> x1, blocking collectives: none -> 60.1 us  [shards(): row_sums = lax.psum(partial_sums, 'gx')]
    dot_general x4, matrix products: 24.6 us -> 66.7 us  [box_band(): jnp.einsum('qtap,pc->qtac', along_z, plane_matrix(half_width), precision=...]
    dot_general x4, matrix products: 21.6 us -> 62 us  [box_band(): jnp.einsum('az,qtzp->qtap', band_matrix(half_width), columns, precision=H...]
    convert_element_type x1, local copies, waits for them, and re-layouts: 6.25 us -> 34.8 us  [quantities(): tiles.astype(jnp.float32)]
  transfers between devices with their start and end apart: 6 -> 5, of which waited for: 4 -> 3; matrix products, arithmetic and copies ran while one was open for 6% -> 10% of each run, Pallas kernels for 0% -> 0%
where the time goes in v1:
time: 681 us; the launch traced here: 669 us
  local copies, waits for them, and re-layouts  322 us (47%)
  matrix products  134 us (20%)
  other arithmetic  107 us (16%)
  blocking collectives  86.8 us (13%)
  starting transfers between devices  12 us (2%)
    gather x100, local copies, waits for them, and re-layouts  150 us
    dot_general x4, matrix products, box_band(): jnp.einsum('qtap,pc->qtac', along_z, plane_matrix(half_width), precision=...  66.7 us
    concatenate x1, other arithmetic, shards(): padded = jnp.concatenate([padded[:, -HW:], padded, padded[:, :HW]], axis=1)  65.7 us
    dot_general x4, matrix products, box_band(): jnp.einsum('az,qtzp->qtap', band_matrix(half_width), columns, precision=H...  62 us
    psum x1, blocking collectives, shards(): row_sums = lax.psum(partial_sums, 'gx')  60.1 us
    unnamed x82, local copies, waits for them, and re-layouts  47.2 us
    another operation x36, local copies, waits for them, and re-layouts, closure_blocks(): stacked = jnp.stack(components, axis=0)  43.8 us
    convert_element_type x1, local copies, waits for them, and re-layouts, quantities(): tiles.astype(jnp.float32)  34.8 us
  transfers between devices with their start and end apart: 5, of which 3 were waited for; matrix products, arithmetic and copies ran while one was open for 10% of the time, Pallas kernels for 0%

profile of v1, /device:TPU:1, one launch (start us, length us, event | category | flops | bytes accessed | tf_op | source)
XLA Modules:
  0.0 669.2 jit_solution(8633491377304584524)
XLA Ops:
  9.0 15.6 %copy.112 = bf16[10,32,64,128]{2,1,3,0:T(8,128)(2,1)} copy(bf16[10,32,64,128]{3,2,1,0:T(8,128)(2,1)} %param.4) | data formatting | bytes 10485760 | tf_op args[0]
  57.0 8.6 %copy.111 = bf16[10,32,4,128]{2,1,3,0:T(8,128)(2,1)} copy(bf16[10,32,4,128]{3,1,2,0:T(8,128)(2,1)} %collective-permute-done) | data formatting | bytes 655360 | tf_op jit(solution)/shard_map/ppermute | solution.py:20
  65.6 8.8 %copy.113 = bf16[10,32,4,128]{2,1,3,0:T(8,128)(2,1)} copy(bf16[10,32,4,128]{3,1,2,0:T(8,128)(2,1)} %collective-permute-done.1) | data formatting | bytes 655360 | tf_op jit(solution)/shard_map/ppermute | solution.py:23
  85.7 65.7 %fusion = bf16[10,40,72,136]{2,1,3,0:T(8,128)(2,1)} fusion(bf16[10,32,72,4]{2,1,3,0:T(8,128)(2,1)S(1)} %collective-permute-done.3, bf16[10,32,72,4]{2,1,3,0:T(8,128)(2,1)S(1)} %collective-permute-done.2, bf16[10,32,4,128]{2,1,3,0:T(8,128)(2,1)S(1)} %copy-done.1, bf16[10,32,64,128]{2,1,3,0:T(8,128)(2,1)} %copy.112, bf16[10,32,4,128]{2,1,3,0:T(8,128)(2,1)S(1)} %bitcast.309), kind=kLoop, calls=%fused_computation.10 | loop fusion | flops 117504000 | bytes 14100480 | tf_op jit(solution)/shard_map/concatenate | solution.py:134
  151.5 150.7 %while.1 = (s32[]{:T(128)}, bf16[10,40,72,136]{2,1,3,0:T(8,128)(2,1)}, s32[20,4]{0,1:T(4,128)S(1)}, bf16[20,10,24,24,24]{4,3,2,1,0:T(8,128)(2,1)}, s32[]{:T(128)}) while((s32[]{:T(128)}, bf16[10,40,72,136]{2,1,3,0:T(8,128)(2,1)}, s32[20,4]{0,1:T(4,128)S(1)}, bf16[20,10,24,24,24]{4,3,2,1,0:T(8,128)(2,1)}, s32[]{:T(128)}) %tuple.64), condition=%wide.while_cond, body=%wide.while_body.sunk | while | flops 2 | bytes 2857605 | solution.py:114
  152.1 4.5 constant_dynamic-slice_fusion.8
  167.0 4.5 constant_dynamic-slice_fusion.8
  182.0 4.5 constant_dynamic-slice_fusion.8
  189.5 4.5 constant_dynamic-slice_fusion.8
  197.2 4.5 constant_dynamic-slice_fusion.8
  204.7 4.5 constant_dynamic-slice_fusion.8
  212.2 4.5 constant_dynamic-slice_fusion.8
  219.8 4.5 constant_dynamic-slice_fusion.8
  227.3 4.5 constant_dynamic-slice_fusion.8
  234.9 4.5 constant_dynamic-slice_fusion.8
  242.4 4.5 constant_dynamic-slice_fusion.8
  249.9 4.5 constant_dynamic-slice_fusion.8
  257.5 4.5 constant_dynamic-slice_fusion.8
  265.1 4.5 constant_dynamic-slice_fusion.8
  272.6 4.5 constant_dynamic-slice_fusion.8
  280.2 4.5 constant_dynamic-slice_fusion.8
  302.2 34.8 %reshape.787 = f32[20,10,24,576]{3,2,1,0:T(8,128)} reshape(bf16[20,10,24,24,24]{4,3,2,1,0:T(8,128)(2,1)} %get-tuple-element.9) | data formatting | bytes 16588800 | tf_op jit(solution)/shard_map/convert_element_type | solution.py:52
  347.6 15.7 %fusion.112 = f32[17,20,576,16]{2,3,1,0:T(8,128)} fusion(f32[17,20,24,576]{3,2,1,0:T(8,128)S(1)} %multiply_dynamic-update-slice_fusion), kind=kOutput, calls=%fused_computation.269 | convolution fusion | flops 902432640 | bytes 31334400 | tf_op jit(solution)/shard_map/az,qtzp->qtap/dot_general | solution.py:45
  363.3 16.5 %fusion.8 = f32[17,20,16,256]{3,2,1,0:T(8,128)S(1)} fusion(f32[17,20,576,16]{2,3,1,0:T(8,128)} %fusion.112, f32[576,256]{0,1:T(8,128)S(1)} %copy-done.5), kind=kOutput, calls=%fused_computation.25 | convolution fusion | flops 9625927680 | bytes 18694144 | tf_op jit(solution)/shard_map/qtap,pc->qtac/dot_general | solution.py:46
  381.7 15.4 %fusion.110 = f32[17,20,576,16]{2,3,1,0:T(8,128)} fusion(f32[17,20,24,576]{3,2,1,0:T(8,128)S(1)} %multiply_dynamic-update-slice_fusion), kind=kOutput, calls=%fused_computation.267 | convolution fusion | flops 902432640 | bytes 31334400 | tf_op jit(solution)/shard_map/az,qtzp->qtap/dot_general | solution.py:45
  397.2 16.9 %fusion.6 = f32[17,20,16,256]{3,2,1,0:T(8,128)S(1)} fusion(f32[17,20,576,16]{2,3,1,0:T(8,128)} %fusion.110, f32[576,256]{0,1:T(8,128)S(1)} %copy-done.4), kind=kOutput, calls=%fused_computation.23 | convolution fusion | flops 9625927680 | bytes 18694144 | tf_op jit(solution)/shard_map/qtap,pc->qtac/dot_general | solution.py:46
  416.7 15.4 %fusion.108 = f32[17,20,576,16]{2,3,1,0:T(8,128)} fusion(f32[17,20,24,576]{3,2,1,0:T(8,128)S(1)} %multiply_dynamic-update-slice_fusion), kind=kOutput, calls=%fused_computation.265 | convolution fusion | flops 902432640 | bytes 31334400 | tf_op jit(solution)/shard_map/az,qtzp->qtap/dot_general | solution.py:45
  432.1 16.7 %fusion.4 = f32[17,20,16,256]{3,2,1,0:T(8,128)S(1)} fusion(f32[17,20,576,16]{2,3,1,0:T(8,128)} %fusion.108, f32[576,256]{0,1:T(8,128)S(1)} %copy-done.3), kind=kOutput, calls=%fused_computation.21 | convolution fusion | flops 9625927680 | bytes 18694144 | tf_op jit(solution)/shard_map/qtap,pc->qtac/dot_general | solution.py:46
  451.4 15.4 %fusion.106 = f32[17,20,576,16]{2,3,1,0:T(8,128)} fusion(f32[17,20,24,576]{3,2,1,0:T(8,128)S(1)} %multiply_dynamic-update-slice_fusion), kind=kOutput, calls=%fused_computation.263 | convolution fusion | flops 902432640 | bytes 31334400 | tf_op jit(solution)/shard_map/az,qtzp->qtap/dot_general | solution.py:45
  466.8 16.7 %fusion.2 = f32[17,20,16,256]{3,2,1,0:T(8,128)S(1)} fusion(f32[17,20,576,16]{2,3,1,0:T(8,128)} %fusion.106, f32[576,256]{0,1:T(8,128)S(1)} %copy-done.2), kind=kOutput, calls=%fused_computation.19 | convolution fusion | flops 9625927680 | bytes 18694144 | tf_op jit(solution)/shard_map/qtap,pc->qtac/dot_general | solution.py:46
  580.7 60.1 %psum.7 = f32[4,1024]{1,0:T(4,128)S(1)} all-reduce(f32[4,1024]{1,0:T(4,128)S(1)} %reshape.691), channel_id=1, replica_groups=mesh['gx'=16,'gy'=8] {'gx'}, use_global_device_ids=true, to_apply=%region_13.14 | all-reduce | flops 4096 | bytes 32768 | tf_op jit(solution)/shard_map/psum | solution.py:188
  640.8 26.7 %all-gather = f32[8,4,1024]{2,1,0:T(4,128)S(1)} all-gather(f32[1,4,1024]{2,1,0:T(4,128)S(1)} %bitcast.314), channel_id=1, replica_groups=mesh['gx'=16,'gy'=8] {'gy'}, dimensions={0}, use_global_device_ids=true | all-gather | bytes 147456 | tf_op jit(solution)/shard_map/all_gather | solution.py:189
  (321 shorter events, 246.2 us)
Async XLA Ops:
  2.3 54.6 %collective-permute-start = (bf16[10,32,4,128]{3,1,2,0:T(8,128)(2,1)S(1)}, bf16[10,32,4,128]{3,1,2,0:T(8,128)(2,1)}, u32[]{:S(2)}, u32[]{:S(2)}) collective-permute-start(bf16[10,32,4,128]{3,1,2,0:T(8,128)(2,1)S(1)} %copy.158), channel_id=1, source_target_pairs={{0,8},{8,16},{16,24},{24,32},{32,40},{40,48},{48,56},{56,64},{64,7... | collective-permute-start | bytes 983048 | tf_op jit(solution)/shard_map/ppermute | solution.py:20
  5.3 60.3 %collective-permute-start.1 = (bf16[10,32,4,128]{3,1,2,0:T(8,128)(2,1)}, bf16[10,32,4,128]{3,1,2,0:T(8,128)(2,1)}, u32[]{:S(2)}, u32[]{:S(2)}) collective-permute-start(bf16[10,32,4,128]{3,1,2,0:T(8,128)(2,1)} %copy.159), channel_id=1, source_target_pairs={{8,0},{16,8},{24,16},{32,24},{40,32},{48,40},{56,48},{64,56},{72,6... | collective-permute-start | bytes 983048 | tf_op jit(solution)/shard_map/ppermute | solution.py:23
  9.0 22.9 %copy-start.10 = (s32[8,16,20]{2,1,0:T(8,128)S(1)}, s32[8,16,20]{2,1,0:T(8,128)}, u32[]{:S(2)}) copy-start(s32[8,16,20]{2,1,0:T(8,128)} %param.5) | copy-start | bytes 30724
  50.2 3.7 copy-start.18
  65.6 20.1 %slice-start = ((s8[10485760]{0:T(1024)(128)(4,1)}), s8[2097152]{0:T(1024)(128)(4,1)S(1)}, s32[]{:S(2)}) async-start(s8[10485760]{0:T(1024)(128)(4,1)} %bitcast.308), calls=%async_computation.1 | async-start | bytes 4194304
  74.4 11.4 %slice-start.1 = ((s8[10485760]{0:T(1024)(128)(4,1)}), s8[4194304]{0:T(1024)(128)(4,1)S(1)}, s32[]{:S(2)}) async-start(s8[10485760]{0:T(1024)(128)(4,1)} %bitcast.308), calls=%async_computation.2 | async-start | bytes 8388608
  74.4 11.4 %slice-start.2 = ((s8[10485760]{0:T(1024)(128)(4,1)}), s8[4194304]{0:T(1024)(128)(4,1)S(1)}, s32[]{:S(2)}) async-start(s8[10485760]{0:T(1024)(128)(4,1)} %bitcast.308), calls=%async_computation.3 | async-start | bytes 8388608
  74.4 11.4 %copy-start.1 = (bf16[10,32,4,128]{2,1,3,0:T(8,128)(2,1)S(1)}, bf16[10,32,4,128]{2,1,3,0:T(8,128)(2,1)}, u32[]{:S(2)}) copy-start(bf16[10,32,4,128]{2,1,3,0:T(8,128)(2,1)} %copy.113) | copy-start | bytes 983044
  76.6 6.6 collective-permute-start.2
  79.2 6.5 collective-permute-start.3
  337.0 9.1 %copy-start = (f32[20,10,24,576]{3,2,1,0:T(8,128)S(1)}, f32[20,10,24,576]{3,2,1,0:T(8,128)}, u32[]{:S(2)}) copy-start(f32[20,10,24,576]{3,2,1,0:T(8,128)} %reshape.787) | copy-start | bytes 33177604
  347.6 15.7 %copy-start.5 = (f32[576,256]{0,1:T(8,128)S(1)}, f32[576,256]{0,1:T(8,128)}, u32[]{:S(2)}) copy-start(f32[576,256]{0,1:T(8,128)} %reshape.680) | copy-start | bytes 1769476
  381.7 15.4 %copy-start.4 = (f32[576,256]{0,1:T(8,128)S(1)}, f32[576,256]{0,1:T(8,128)}, u32[]{:S(2)}) copy-start(f32[576,256]{0,1:T(8,128)} %reshape.681) | copy-start | bytes 1769476
  416.7 15.4 %copy-start.3 = (f32[576,256]{0,1:T(8,128)S(1)}, f32[576,256]{0,1:T(8,128)}, u32[]{:S(2)}) copy-start(f32[576,256]{0,1:T(8,128)} %reshape.682) | copy-start | bytes 1769476
  451.4 15.4 %copy-start.2 = (f32[576,256]{0,1:T(8,128)S(1)}, f32[576,256]{0,1:T(8,128)}, u32[]{:S(2)}) copy-start(f32[576,256]{0,1:T(8,128)} %reshape.683) | copy-start | bytes 1769476
  491.6 12.9 %copy-start.12 = (s32[256]{0:T(256)S(1)}, s32[256]{0:T(256)}, u32[]{:S(2)}) copy-start(s32[256]{0:T(256)} %get-tuple-element.90) | copy-start | bytes 3076
  491.6 12.9 %copy-start.13 = (s32[256]{0:T(256)S(1)}, s32[256]{0:T(256)}, u32[]{:S(2)}) copy-start(s32[256]{0:T(256)} %get-tuple-element.91) | copy-start | bytes 3076
  491.6 12.9 %copy-start.14 = (s32[256]{0:T(256)S(1)}, s32[256]{0:T(256)}, u32[]{:S(2)}) copy-start(s32[256]{0:T(256)} %get-tuple-element.92) | copy-start | bytes 3076
  491.6 12.9 %copy-start.15 = (s32[256]{0:T(256)S(1)}, s32[256]{0:T(256)}, u32[]{:S(2)}) copy-start(s32[256]{0:T(256)} %get-tuple-element.93) | copy-start | bytes 3076
  491.6 12.9 %copy-start.16 = (pred[256]{0:T(512)(128)(4,1)S(1)}, pred[256]{0:T(512)(128)(4,1)}, u32[]{:S(2)}) copy-start(pred[256]{0:T(512)(128)(4,1)} %get-tuple-element.88) | copy-start | bytes 772
  491.6 12.9 %copy-start.17 = (pred[256]{0:T(512)(128)(4,1)S(1)}, pred[256]{0:T(512)(128)(4,1)}, u32[]{:S(2)}) copy-start(pred[256]{0:T(512)(128)(4,1)} %get-tuple-element.89) | copy-start | bytes 772
  505.5 9.8 %copy-start.8 = (f32[1,20,16,256]{3,2,1,0:T(8,128)S(1)}, f32[1,20,16,256]{3,2,1,0:T(8,128)}, u32[]{:S(2)}) copy-start(f32[1,20,16,256]{3,2,1,0:T(8,128)} %get-tuple-element.60) | copy-start | bytes 983044
  525.3 9.8 %copy-start.7 = (f32[1,20,16,256]{3,2,1,0:T(8,128)S(1)}, f32[1,20,16,256]{3,2,1,0:T(8,128)}, u32[]{:S(2)}) copy-start(f32[1,20,16,256]{3,2,1,0:T(8,128)} %get-tuple-element.68) | copy-start | bytes 983044
  545.5 9.8 %copy-start.6 = (f32[1,20,16,256]{3,2,1,0:T(8,128)S(1)}, f32[1,20,16,256]{3,2,1,0:T(8,128)}, u32[]{:S(2)}) copy-start(f32[1,20,16,256]{3,2,1,0:T(8,128)} %get-tuple-element.76) | copy-start | bytes 983044
  560.3 11.7 %copy-start.11 = (s32[1,16,20]{2,1,0:T(8,128)S(1)}, s32[1,16,20]{2,1,0:T(8,128)}, u32[]{:S(2)}) copy-start(s32[1,16,20]{2,1,0:T(8,128)} %constant_dynamic-slice_fusion.2) | copy-start | bytes 3844
  567.8 11.5 %all-to-all-start = ((f32[16,2,2048]{2,1,0:T(2,128)}), f32[16,2,2048]{2,1,0:T(2,128)S(1)}, u32[]{:S(2)}, u32[]{:S(2)}) async-start(f32[16,2,2048]{2,1,0:T(2,128)} %reshape.685), calls=%async_computation | async-start | bytes 524288 | tf_op jit(solution)/shard_map/all_to_all | solution.py:170
  580.2 88.5 %copy-start.9 = (f32[8,2048]{1,0:T(8,128)}, f32[8,2048]{1,0:T(8,128)S(1)}, u32[]{:S(2)}) copy-start(f32[8,2048]{1,0:T(8,128)S(1)} %gather_fusion) | copy-start | bytes 196612

commit v2 on v1

--- a/solution.py
+++ b/solution.py
@@ -94,12 +94,40 @@
     return blocks.reshape(8, tile_count, sub_edge**3)
 
 
+def plane_ones(half_width):
+    span = TE + 2 * HW
+    row_index = lax.broadcasted_iota(jnp.int32, (TE, span), 0)
+    column_index = lax.broadcasted_iota(jnp.int32, (TE, span), 1)
+    inside = (jnp.abs(column_index - row_index - HW) <= half_width).astype(jnp.float32)
+    return (
+        jnp.einsum("ax,by->xyab", inside, inside, precision=HIGHEST)
+        .reshape(span * span, TE * TE)
+        .astype(jnp.bfloat16)
+    )
+
+
+def split_three(values):
+    high = lax.reduce_precision(values, exponent_bits=8, mantissa_bits=7)
+    rest = values - high
+    middle = lax.reduce_precision(rest, exponent_bits=8, mantissa_bits=7)
+    low = rest - middle
+    return jnp.stack([high, middle, low], axis=0).astype(jnp.bfloat16)
+
+
 def tile_statistics(tiles):
     total_tiles = tiles.shape[0]
     columns = quantities(tiles)
     results = []
     for half_width in range(1, HW + 1):
-        results.append(closure_blocks(box_band(columns, half_width)))
+        window = 2 * half_width + 1
+        depth_sum = columns[:, :, HW - half_width : HW - half_width + TE]
+        for step in range(1, window):
+            start = HW - half_width + step
+            depth_sum = depth_sum + columns[:, :, start : start + TE]
+        pieces = split_three(depth_sum)
+        plane = jnp.dot(pieces, plane_ones(half_width), preferred_element_type=jnp.float32)
+        smoothed = (plane[0] + plane[1] + plane[2]) / float(window**3)
+        results.append(closure_blocks(smoothed))
     mapped = jnp.stack(results, axis=0)
     return jnp.transpose(mapped, (2, 0, 1, 3)).reshape(total_tiles, HW * 8 * (TE // 4) ** 3)
 
@@ -169,26 +197,19 @@
     )
     incoming = lax.all_to_all(outgoing, "gx", split_axis=0, concat_axis=0, tiled=True)
     statistics = incoming.reshape(groups_x * CAP, stat_length)[take_slot]
-    tile_means = jnp.mean(
-        statistics.reshape(per_filter, HW * 8, stat_length // (HW * 8)), axis=2
-    )
-    tile_x = take_source * across_x + take_tile // across_y % across_x
-    tile_y = self_row * across_y + take_tile % across_y
+    own_means = jnp.where(
+        is_listed[:, None],
+        jnp.mean(own_statistics.reshape(list_length, HW * 8, stat_length // (HW * 8)), axis=2),
+        0.0,
+    )
+    every_means = lax.all_gather(own_means, ("gx", "gy"), axis=0, tiled=False)
+    every_means = jnp.transpose(
+        every_means.reshape(groups_x, groups_y, list_length, HW * 8), (1, 0, 2, 3)
+    ).reshape(groups_y * groups_x * list_length, HW * 8)
     pencils = pencil_order.shape[0]
     coarse_x = across_x * groups_x // 2
     per_row = pencils // groups_y
-    local_pencil = tile_y // 2 - self_row * per_row
-    cell_no = local_pencil * coarse_x + tile_x // 2
-    placing = (
-        lax.broadcasted_iota(jnp.int32, (per_row * coarse_x, per_filter), 0) == cell_no[None, :]
-    ).astype(jnp.float32)
-    partial_sums = jnp.dot(
-        placing, tile_means, precision=HIGHEST, preferred_element_type=jnp.float32
-    ).reshape(per_row, coarse_x * HW * 8)
-    row_sums = lax.psum(partial_sums, "gx")
-    all_rows = lax.all_gather(row_sums, "gy", axis=0, tiled=True)
     row_pencils = lax.dynamic_slice_in_dim(pencil_order, self_row * per_row, per_row)
-    own_rows = all_rows[row_pencils]
     every_tile = dense_list.reshape(-1)
     every_valid = every_tile >= 0
     every_group = lax.broadcasted_iota(jnp.int32, dense_list.shape, 0).reshape(-1)
@@ -200,9 +221,10 @@
         every_x[:, None] == lax.broadcasted_iota(jnp.int32, (every_x.shape[0], coarse_x), 1)
     ).astype(jnp.float32)
     tile_counts = jnp.dot(in_row, in_column, precision=HIGHEST, preferred_element_type=jnp.float32)
-    averaged = (
-        own_rows.reshape(per_row, coarse_x, HW * 8) / jnp.maximum(tile_counts, 1.0)[:, :, None]
-    )
+    cell_sums = jnp.einsum(
+        "rj,jc,jk->rck", in_row, in_column, every_means, precision=HIGHEST
+    )
+    averaged = cell_sums / jnp.maximum(tile_counts, 1.0)[:, :, None]
     return (statistics, averaged.reshape(per_row, coarse_x * HW * 8))
 
 

time: 681 us -> 761 us (1.12)
  other arithmetic: 107 us -> 301 us
  matrix products: 134 us -> 64 us
  blocking collectives: 86.8 us -> 40.6 us
    another operation x3 -> x14, other arithmetic: 0.42 us -> 155 us  [the longest x5 154 us: split_three(): return jnp.stack([high, middle, low], axis=0).astype(jnp.bfloat16)]
    dot_general x9 -> x5, matrix products: 129 us -> 59.2 us  [the longest x4 58 us: tile_statistics(): jnp.dot(pieces, plane_ones(half_width), preferred_element_type=jnp.float32)]
    psum x1 -> x0, blocking collectives: 60.1 us -> none  [shards(): row_sums = lax.psum(partial_sums, 'gx')]
    div x5 -> x4, other arithmetic: 4.16 us -> 34.5 us  [tile_statistics(): smoothed = (plane[0] + plane[1] + plane[2]) / float(window ** 3)]
    all_gather x1, blocking collectives: 26.7 us -> 40.6 us  [shards(): every_means = lax.all_gather(own_means, ('gx', 'gy'), axis=0, tiled=False)]
    unnamed x12 -> x13, other arithmetic: 1.32 us -> 11.8 us
    unnamed x82 -> x101, local copies, waits for them, and re-layouts: 47.2 us -> 55.8 us
    gather x101 -> x100, local copies, waits for them, and re-layouts: 151 us -> 147 us
  transfers between devices with their start and end apart: 5 -> 5, of which waited for: 3 -> 2; matrix products, arithmetic and copies ran while one was open for 10% -> 7% of each run, Pallas kernels for 0% -> 0%
where the time goes in v2:
time: 761 us; the launch traced here: 749 us
  local copies, waits for them, and re-layouts  320 us (42%)
  other arithmetic  301 us (40%)
  matrix products  64 us (8%)
  blocking collectives  40.6 us (5%)
  starting transfers between devices  14.6 us (2%)
    another operation x5, other arithmetic, split_three(): return jnp.stack([high, middle, low], axis=0).astype(jnp.bfloat16)  154 us
    gather x100, local copies, waits for them, and re-layouts  147 us
    concatenate x1, other arithmetic, shards(): padded = jnp.concatenate([padded[:, -HW:], padded, padded[:, :HW]], axis=1)  65.7 us
    dot_general x4, matrix products, tile_statistics(): jnp.dot(pieces, plane_ones(half_width), preferred_element_type=jnp.float32)  58 us
    unnamed x101, local copies, waits for them, and re-layouts  55.8 us
    another operation x36, local copies, waits for them, and re-layouts, closure_blocks(): stacked = jnp.stack(components, axis=0)  44 us
    all_gather x1, blocking collectives, shards(): every_means = lax.all_gather(own_means, ('gx', 'gy'), axis=0, tiled=False)  40.6 us
    convert_element_type x1, local copies, waits for them, and re-layouts, quantities(): tiles.astype(jnp.float32)  34.8 us
  transfers between devices with their start and end apart: 5, of which 2 were waited for; matrix products, arithmetic and copies ran while one was open for 7% of the time, Pallas kernels for 0%

profile of v2, /device:TPU:1, one launch (start us, length us, event | category | flops | bytes accessed | tf_op | source)
XLA Modules:
  0.0 748.7 jit_solution(6100721995676070267)
XLA Ops:
  2.3 5.8 collective-permute-start.1
  11.6 15.6 %copy.107 = bf16[10,32,64,128]{2,1,3,0:T(8,128)(2,1)} copy(bf16[10,32,64,128]{3,2,1,0:T(8,128)(2,1)} %param.4) | data formatting | bytes 10485760 | tf_op args[0]
  43.5 7.9 %copy.106 = bf16[10,32,4,128]{2,1,3,0:T(8,128)(2,1)} copy(bf16[10,32,4,128]{3,1,2,0:T(8,128)(2,1)S(1)} %collective-permute-done) | data formatting | bytes 655360 | tf_op jit(solution)/shard_map/ppermute | solution.py:20
  51.5 7.8 %copy.108 = bf16[10,32,4,128]{2,1,3,0:T(8,128)(2,1)} copy(bf16[10,32,4,128]{3,1,2,0:T(8,128)(2,1)S(1)} %collective-permute-done.1) | data formatting | bytes 655360 | tf_op jit(solution)/shard_map/ppermute | solution.py:23
  70.5 65.7 %fusion.34 = bf16[10,40,72,136]{2,1,3,0:T(8,128)(2,1)} fusion(bf16[10,32,72,4]{2,1,3,0:T(8,128)(2,1)S(1)} %collective-permute-done.3, bf16[10,32,72,4]{2,1,3,0:T(8,128)(2,1)S(1)} %collective-permute-done.2, bf16[10,32,4,128]{2,1,3,0:T(8,128)(2,1)S(1)} %copy-done.1, bf16[10,32,64,128]{2,1,3,0:T(8,128)(2,1)} %copy.107, bf16[10,32,4,128]{2,1,3,0:T(8,128)(2,1)S(1)} %bitcast.764), kind=kLoop, calls=%fused_computation.59 | loop fusion | flops 117504000 | bytes 14100480 | tf_op jit(solution)/shard_map/concatenate | solution.py:162
  136.2 147.4 %while.1 = (s32[]{:T(128)}, bf16[10,40,72,136]{2,1,3,0:T(8,128)(2,1)}, s32[20,4]{0,1:T(4,128)S(1)}, bf16[20,10,24,24,24]{4,3,2,1,0:T(8,128)(2,1)}, s32[]{:T(128)}) while((s32[]{:T(128)}, bf16[10,40,72,136]{2,1,3,0:T(8,128)(2,1)}, s32[20,4]{0,1:T(4,128)S(1)}, bf16[20,10,24,24,24]{4,3,2,1,0:T(8,128)(2,1)}, s32[]{:T(128)}) %tuple.78), condition=%wide.while_cond, body=%wide.while_body.sunk | while | flops 2 | bytes 2857105 | solution.py:142
  136.9 4.3 constant_dynamic-slice_fusion.8
  144.2 4.3 constant_dynamic-slice_fusion.8
  180.8 4.3 constant_dynamic-slice_fusion.8
  188.2 4.3 constant_dynamic-slice_fusion.8
  195.6 4.3 constant_dynamic-slice_fusion.8
  210.3 4.3 constant_dynamic-slice_fusion.8
  225.1 4.3 constant_dynamic-slice_fusion.8
  232.5 4.3 constant_dynamic-slice_fusion.8
  239.9 4.3 constant_dynamic-slice_fusion.8
  269.5 4.3 constant_dynamic-slice_fusion.8
  283.6 34.8 %reshape.866 = f32[20,10,24,576]{3,2,1,0:T(8,128)} reshape(bf16[20,10,24,24,24]{4,3,2,1,0:T(8,128)(2,1)} %get-tuple-element.9) | data formatting | bytes 16588800 | tf_op jit(solution)/shard_map/convert_element_type | solution.py:52
  346.9 40.9 %fusion.42 = (bf16[1,17,20,16,576]{4,3,2,1,0:T(8,128)(2,1)}, f32[17,20,16,576]{3,2,1,0:T(8,128)}) fusion(f32[17,20,24,576]{3,2,1,0:T(8,128)} %multiply_dynamic-update-slice_fusion), kind=kLoop, calls=%fused_computation.77 | loop fusion | flops 18800640 | bytes 81469440 | tf_op jit(solution)/shard_map/stack | solution.py:114
  387.7 10.8 %fusion.43 = (bf16[1,17,20,16,576]{4,3,2,1,0:T(8,128)(2,1)}, bf16[1,17,20,16,576]{4,3,2,1,0:T(8,128)(2,1)}) fusion(f32[17,20,16,576]{3,2,1,0:T(8,128)} %get-tuple-element.43), kind=kLoop, calls=%fused_computation.78 | loop fusion | flops 18800640 | bytes 25067520 | tf_op jit(solution)/shard_map/stack | solution.py:114
  398.6 14.4 %fusion.6 = f32[3,17,20,16,256]{4,3,2,1,0:T(8,128)} fusion(bf16[1,17,20,16,576]{4,3,2,1,0:T(8,128)(2,1)} %get-tuple-element.62, bf16[1,17,20,16,576]{4,3,2,1,0:T(8,128)(2,1)} %get-tuple-element.61, bf16[1,17,20,16,576]{4,3,2,1,0:T(8,128)(2,1)} %get-tuple-element.42, bf16[576,256]{0,1:T(8,128)(2,1)S(1)} %convert_element_type.77), kind=kOutput, calls=%fused_computation.12 | convolution fusion | flops 4831764480 | bytes 35807232 | tf_op jit(solution)/shard_map/dot_general | solution.py:128
  412.9 7.9 %fusion.50 = f32[1,17,20,16,256]{4,3,2,1,0:T(8,128)S(1)} fusion(f32[3,17,20,16,256]{4,3,2,1,0:T(8,128)} %fusion.6), kind=kLoop, calls=%fused_computation.90 | loop fusion | flops 4177920 | bytes 22282240 | tf_op jit(solution)/shard_map/div | solution.py:129
  423.6 75.2 %fusion.40 = (bf16[1,17,20,16,576]{4,3,2,1,0:T(8,128)(2,1)}, f32[17,20,16,576]{3,2,1,0:T(8,128)}, bf16[1,17,20,16,576]{4,3,2,1,0:T(8,128)(2,1)}, f32[17,20,16,57...) fusion(f32[17,20,24,576]{3,2,1,0:T(8,128)} %multiply_dynamic-update-slice_fusion), kind=kLoop, calls=%fused_computation.75 | loop fusion | flops 68935680 | bytes 169205760 | tf_op jit(solution)/shard_map/stack | solution.py:114
  498.8 10.8 %fusion.47 = (bf16[1,17,20,16,576]{4,3,2,1,0:T(8,128)(2,1)}, bf16[1,17,20,16,576]{4,3,2,1,0:T(8,128)(2,1)}) fusion(f32[17,20,16,576]{3,2,1,0:T(8,128)} %get-tuple-element.58), kind=kLoop, calls=%fused_computation.82 | loop fusion | flops 18800640 | bytes 25067520 | tf_op jit(solution)/shard_map/stack | solution.py:114
  509.6 14.7 %fusion.18 = f32[3,17,20,16,256]{4,3,2,1,0:T(8,128)} fusion(bf16[1,17,20,16,576]{4,3,2,1,0:T(8,128)(2,1)} %get-tuple-element.66, bf16[1,17,20,16,576]{4,3,2,1,0:T(8,128)(2,1)} %get-tuple-element.65, bf16[1,17,20,16,576]{4,3,2,1,0:T(8,128)(2,1)} %get-tuple-element.57, bf16[576,256]{0,1:T(8,128)(2,1)S(1)} %copy-done.13), kind=kOutput, calls=%fused_computation.24 | convolution fusion | flops 4831764480 | bytes 35807232 | tf_op jit(solution)/shard_map/dot_general | solution.py:128
  524.3 10.8 %fusion.48 = f32[1,17,20,16,256]{4,3,2,1,0:T(8,128)} fusion(f32[3,17,20,16,256]{4,3,2,1,0:T(8,128)} %fusion.18), kind=kLoop, calls=%fused_computation.84 | loop fusion | flops 4177920 | bytes 22282240 | tf_op jit(solution)/shard_map/div | solution.py:129
  541.9 15.8 %fusion.41 = (bf16[1,17,20,16,576]{4,3,2,1,0:T(8,128)(2,1)}, bf16[1,17,20,16,576]{4,3,2,1,0:T(8,128)(2,1)}, bf16[1,17,20,16,576]{4,3,2,1,0:T(8,128)(2,1)}, bf16[1,17,20,16,576]{4,3,2,1,0:T(8,128)(2,1)}) fusion(f32[17,20,16,576]{3,2,1,0:T(8,128)S(1)} %bitcast.766, f32[17,20,16,576]{3,2,1,0:T(8,128)} %get-tuple-element.56), kind=kLoop, calls=%fused_computation.76 | loop fusion | flops 37601280 | bytes 50135040 | tf_op jit(solution)/shard_map/stack | solution.py:114
  557.7 14.3 %fusion = f32[3,17,20,16,256]{4,3,2,1,0:T(8,128)} fusion(bf16[1,17,20,16,576]{4,3,2,1,0:T(8,128)(2,1)} %get-tuple-element.60, bf16[1,17,20,16,576]{4,3,2,1,0:T(8,128)(2,1)} %get-tuple-element.59, bf16[1,17,20,16,576]{4,3,2,1,0:T(8,128)(2,1)} %get-tuple-element.40, bf16[576,256]{0,1:T(8,128)(2,1)S(1)} %copy-done.12), kind=kOutput, calls=%fused_computation.6 | convolution fusion | flops 4831764480 | bytes 35807232 | tf_op jit(solution)/shard_map/dot_general | solution.py:128
  572.1 7.9 %fusion.51 = f32[1,17,20,16,256]{4,3,2,1,0:T(8,128)S(1)} fusion(f32[3,17,20,16,256]{4,3,2,1,0:T(8,128)} %fusion), kind=kLoop, calls=%fused_computation.93 | loop fusion | flops 4177920 | bytes 22282240 | tf_op jit(solution)/shard_map/div | solution.py:129
  582.8 14.6 %fusion.12 = f32[3,17,20,16,256]{4,3,2,1,0:T(8,128)} fusion(bf16[1,17,20,16,576]{4,3,2,1,0:T(8,128)(2,1)} %get-tuple-element.110, bf16[1,17,20,16,576]{4,3,2,1,0:T(8,128)(2,1)} %get-tuple-element.111, bf16[1,17,20,16,576]{4,3,2,1,0:T(8,128)(2,1)} %get-tuple-element.55, bf16[576,256]{0,1:T(8,128)(2,1)S(1)} %copy-done.11), kind=kOutput, calls=%fused_computation.18 | convolution fusion | flops 4831764480 | bytes 35807232 | tf_op jit(solution)/shard_map/dot_general | solution.py:128
  597.4 7.9 %fusion.49 = f32[1,17,20,16,256]{4,3,2,1,0:T(8,128)S(1)} fusion(f32[3,17,20,16,256]{4,3,2,1,0:T(8,128)} %fusion.12), kind=kLoop, calls=%fused_computation.87 | loop fusion | flops 4177920 | bytes 22282240 | tf_op jit(solution)/shard_map/div | solution.py:129
  693.2 6.2 all-to-all-start
  699.5 40.6 %all_gather.4 = f32[128,20,32]{2,1,0:T(8,128)} all-gather(f32[1,20,32]{2,1,0:T(8,128)S(1)} %copy.129), channel_id=1, replica_groups=mesh['gx'=16,'gy'=8] {'gx','gy'}, dimensions={0}, use_global_device_ids=true | all-gather | bytes 330240 | tf_op jit(solution)/shard_map/all_gather | solution.py:205
  (339 shorter events, 273.0 us)
Async XLA Ops:
  2.3 49.1 %collective-permute-start.1 = (bf16[10,32,4,128]{3,1,2,0:T(8,128)(2,1)S(1)}, bf16[10,32,4,128]{3,1,2,0:T(8,128)(2,1)S(1)}, u32[]{:S(2)}, u32[]{:S(2)}) collective-permute-start(bf16[10,32,4,128]{3,1,2,0:T(8,128)(2,1)S(1)} %copy.153), channel_id=1, source_target_pairs={{8,0},{16,8},{24,16},{32,24},{40,32},{48,40},{56,48},{64,56},{72,6... | collective-permute-start | bytes 983048 | tf_op jit(solution)/shard_map/ppermute | solution.py:23
  8.2 35.3 %collective-permute-start = (bf16[10,32,4,128]{3,1,2,0:T(8,128)(2,1)S(1)}, bf16[10,32,4,128]{3,1,2,0:T(8,128)(2,1)S(1)}, u32[]{:S(2)}, u32[]{:S(2)}) collective-permute-start(bf16[10,32,4,128]{3,1,2,0:T(8,128)(2,1)S(1)} %copy.152), channel_id=1, source_target_pairs={{0,8},{8,16},{16,24},{24,32},{32,40},{40,48},{48,56},{56,64},{64,7... | collective-permute-start | bytes 983048 | tf_op jit(solution)/shard_map/ppermute | solution.py:20
  11.6 17.0 %copy-start.14 = (s32[8,16,20]{2,1,0:T(8,128)S(1)}, s32[8,16,20]{2,1,0:T(8,128)}, u32[]{:S(2)}) copy-start(s32[8,16,20]{2,1,0:T(8,128)} %param.5) | copy-start | bytes 30724
  31.4 7.6 %copy-start.23 = (s32[32]{0:T(128)S(1)}, s32[32]{0:T(128)}, u32[]{:S(2)}) copy-start(s32[32]{0:T(128)} %param.7) | copy-start | bytes 388
  51.5 19.0 %slice-start = ((s8[10485760]{0:T(1024)(128)(4,1)}), s8[2097152]{0:T(1024)(128)(4,1)S(1)}, s32[]{:S(2)}) async-start(s8[10485760]{0:T(1024)(128)(4,1)} %bitcast.763), calls=%async_computation.1 | async-start | bytes 4194304
  59.2 11.2 %slice-start.1 = ((s8[10485760]{0:T(1024)(128)(4,1)}), s8[4194304]{0:T(1024)(128)(4,1)S(1)}, s32[]{:S(2)}) async-start(s8[10485760]{0:T(1024)(128)(4,1)} %bitcast.763), calls=%async_computation.2 | async-start | bytes 8388608
  59.2 11.2 %slice-start.2 = ((s8[10485760]{0:T(1024)(128)(4,1)}), s8[4194304]{0:T(1024)(128)(4,1)S(1)}, s32[]{:S(2)}) async-start(s8[10485760]{0:T(1024)(128)(4,1)} %bitcast.763), calls=%async_computation.3 | async-start | bytes 8388608
  59.2 11.2 %copy-start.1 = (bf16[10,32,4,128]{2,1,3,0:T(8,128)(2,1)S(1)}, bf16[10,32,4,128]{2,1,3,0:T(8,128)(2,1)}, u32[]{:S(2)}) copy-start(bf16[10,32,4,128]{2,1,3,0:T(8,128)(2,1)} %copy.108) | copy-start | bytes 983044
  61.5 6.5 collective-permute-start.2
  64.0 6.5 collective-permute-start.3
  318.4 15.5 %copy-start = (f32[20,10,24,576]{3,2,1,0:T(8,128)S(1)}, f32[20,10,24,576]{3,2,1,0:T(8,128)}, u32[]{:S(2)}) copy-start(f32[20,10,24,576]{3,2,1,0:T(8,128)} %reshape.866) | copy-start | bytes 33177604
  498.8 10.8 %copy-start.13 = (bf16[576,256]{0,1:T(8,128)(2,1)S(1)}, bf16[576,256]{0,1:T(8,128)(2,1)}, u32[]{:S(2)}) copy-start(bf16[576,256]{0,1:T(8,128)(2,1)} %convert_element_type.83) | copy-start | bytes 884740
  524.3 17.5 %slice-start.3 = ((s8[13926400]{0:T(1024)(128)(4,1)}), s8[1343488]{0:T(1024)(128)(4,1)S(1)}, s32[]{:S(2)}) async-start(s8[13926400]{0:T(1024)(128)(4,1)} %bitcast.765), calls=%async_computation.4 | async-start | bytes 2686976
  524.3 17.5 %slice-start.4 = ((s8[13926400]{0:T(1024)(128)(4,1)}), s8[4194304]{0:T(1024)(128)(4,1)S(1)}, s32[]{:S(2)}) async-start(s8[13926400]{0:T(1024)(128)(4,1)} %bitcast.765), calls=%async_computation.5 | async-start | bytes 8388608
  524.3 17.5 %slice-start.5 = ((s8[13926400]{0:T(1024)(128)(4,1)}), s8[4194304]{0:T(1024)(128)(4,1)S(1)}, s32[]{:S(2)}) async-start(s8[13926400]{0:T(1024)(128)(4,1)} %bitcast.765), calls=%async_computation.6 | async-start | bytes 8388608
  535.1 6.8 slice-start.6
  541.9 15.8 %copy-start.12 = (bf16[576,256]{0,1:T(8,128)(2,1)S(1)}, bf16[576,256]{0,1:T(8,128)(2,1)}, u32[]{:S(2)}) copy-start(bf16[576,256]{0,1:T(8,128)(2,1)} %convert_element_type.74) | copy-start | bytes 884740
  605.4 4.7 copy-start.5
  605.4 5.6 copy-start.4
  605.4 6.4 copy-start.3
  605.4 7.2 copy-start.2
  608.2 13.5 %copy-start.16 = (s32[256]{0:T(256)S(1)}, s32[256]{0:T(256)}, u32[]{:S(2)}) copy-start(s32[256]{0:T(256)} %get-tuple-element.114) | copy-start | bytes 3076
  608.2 13.5 %copy-start.17 = (s32[256]{0:T(256)S(1)}, s32[256]{0:T(256)}, u32[]{:S(2)}) copy-start(s32[256]{0:T(256)} %get-tuple-element.115) | copy-start | bytes 3076
  608.2 13.5 %copy-start.18 = (s32[256]{0:T(256)S(1)}, s32[256]{0:T(256)}, u32[]{:S(2)}) copy-start(s32[256]{0:T(256)} %get-tuple-element.112) | copy-start | bytes 3076
  608.2 13.5 %copy-start.19 = (s32[256]{0:T(256)S(1)}, s32[256]{0:T(256)}, u32[]{:S(2)}) copy-start(s32[256]{0:T(256)} %get-tuple-element.113) | copy-start | bytes 3076
  608.2 13.5 %copy-start.20 = (pred[256]{0:T(512)(128)(4,1)S(1)}, pred[256]{0:T(512)(128)(4,1)}, u32[]{:S(2)}) copy-start(pred[256]{0:T(512)(128)(4,1)} %get-tuple-element.108) | copy-start | bytes 772
  608.2 13.5 %copy-start.21 = (pred[256]{0:T(512)(128)(4,1)S(1)}, pred[256]{0:T(512)(128)(4,1)}, u32[]{:S(2)}) copy-start(pred[256]{0:T(512)(128)(4,1)} %get-tuple-element.109) | copy-start | bytes 772
  674.1 17.2 %copy-start.22 = (pred[20]{0:T(512)(128)(4,1)S(1)}, pred[20]{0:T(512)(128)(4,1)}, u32[]{:S(2)}) copy-start(pred[20]{0:T(512)(128)(4,1)} %get-tuple-element.38) | copy-start | bytes 64
  689.5 55.5 %copy-start.24 = (f32[4,32]{1,0:T(4,128)S(1)}, f32[4,32]{1,0:T(4,128)}, u32[]{:S(2)}) copy-start(f32[4,32]{1,0:T(4,128)} %convolution_maximum_fusion) | copy-start | bytes 1540
  690.5 54.6 %copy-start.10 = (f32[2560,32]{0,1:T(8,128)S(1)}, f32[2560,32]{0,1:T(8,128)}, u32[]{:S(2)}) copy-start(f32[2560,32]{0,1:T(8,128)} %fusion.154) | copy-start | bytes 983044
  690.5 54.6 %copy-start.15 = (f32[2560,4]{0,1:T(4,128)S(1)}, f32[2560,4]{0,1:T(4,128)}, u32[]{:S(2)}) copy-start(f32[2560,4]{0,1:T(4,128)} %convert_bitcast_fusion) | copy-start | bytes 122884
  693.2 53.7 %all-to-all-start = ((f32[16,2,2048]{2,1,0:T(2,128)}), f32[16,2,2048]{2,1,0:T(2,128)S(1)}, u32[]{:S(2)}, u32[]{:S(2)}) async-start(f32[16,2,2048]{2,1,0:T(2,128)} %reshape.796), calls=%async_computation | async-start | bytes 524288 | tf_op jit(solution)/shard_map/all_to_all | solution.py:198
  (5 other events, 15.6 us)

commit v3 on v2

--- a/solution.py
+++ b/solution.py
@@ -94,40 +94,12 @@
     return blocks.reshape(8, tile_count, sub_edge**3)
 
 
-def plane_ones(half_width):
-    span = TE + 2 * HW
-    row_index = lax.broadcasted_iota(jnp.int32, (TE, span), 0)
-    column_index = lax.broadcasted_iota(jnp.int32, (TE, span), 1)
-    inside = (jnp.abs(column_index - row_index - HW) <= half_width).astype(jnp.float32)
-    return (
-        jnp.einsum("ax,by->xyab", inside, inside, precision=HIGHEST)
-        .reshape(span * span, TE * TE)
-        .astype(jnp.bfloat16)
-    )
-
-
-def split_three(values):
-    high = lax.reduce_precision(values, exponent_bits=8, mantissa_bits=7)
-    rest = values - high
-    middle = lax.reduce_precision(rest, exponent_bits=8, mantissa_bits=7)
-    low = rest - middle
-    return jnp.stack([high, middle, low], axis=0).astype(jnp.bfloat16)
-
-
 def tile_statistics(tiles):
     total_tiles = tiles.shape[0]
     columns = quantities(tiles)
     results = []
     for half_width in range(1, HW + 1):
-        window = 2 * half_width + 1
-        depth_sum = columns[:, :, HW - half_width : HW - half_width + TE]
-        for step in range(1, window):
-            start = HW - half_width + step
-            depth_sum = depth_sum + columns[:, :, start : start + TE]
-        pieces = split_three(depth_sum)
-        plane = jnp.dot(pieces, plane_ones(half_width), preferred_element_type=jnp.float32)
-        smoothed = (plane[0] + plane[1] + plane[2]) / float(window**3)
-        results.append(closure_blocks(smoothed))
+        results.append(closure_blocks(box_band(columns, half_width)))
     mapped = jnp.stack(results, axis=0)
     return jnp.transpose(mapped, (2, 0, 1, 3)).reshape(total_tiles, HW * 8 * (TE // 4) ** 3)
 

time: 761 us -> 634 us (0.83)
  other arithmetic: 301 us -> 106 us
  matrix products: 64 us -> 135 us
    another operation x14 -> x5, other arithmetic: 155 us -> 1.88 us  [the longest x5 154 us: split_three(): return jnp.stack([high, middle, low], axis=0).astype(jnp.bfloat16)]
    dot_general x4 -> x8, matrix products: 58 us -> 129 us  [the longest x4 66.7 us: box_band(): jnp.einsum('qtap,pc->qtac', along_z, plane_matrix(half_width), precision=...]
    div x4, other arithmetic: 34.5 us -> 3.56 us  [closure_blocks(): components.append(smoothed[12] / solid_mean)]
    unnamed x13 -> x12, other arithmetic: 11.8 us -> 1.32 us
    unnamed x101 -> x83, local copies, waits for them, and re-layouts: 55.8 us -> 47.2 us
  transfers between devices with their start and end apart: 5 -> 5, of which waited for: 2 -> 2; matrix products, arithmetic and copies ran while one was open for 7% -> 11% of each run, Pallas kernels for 0% -> 0%
where the time goes in v3:
time: 634 us; the launch traced here: 621 us
  local copies, waits for them, and re-layouts  321 us (51%)
  matrix products  135 us (21%)
  other arithmetic  106 us (17%)
  blocking collectives  39.9 us (6%)
  starting transfers between devices  12 us (2%)
    gather x100, local copies, waits for them, and re-layouts  151 us
    dot_general x4, matrix products, box_band(): jnp.einsum('qtap,pc->qtac', along_z, plane_matrix(half_width), precision=...  66.7 us
    concatenate x1, other arithmetic, shards(): padded = jnp.concatenate([padded[:, -HW:], padded, padded[:, :HW]], axis=1)  65.8 us
    dot_general x4, matrix products, box_band(): jnp.einsum('az,qtzp->qtap', band_matrix(half_width), columns, precision=H...  62.3 us
    unnamed x83, local copies, waits for them, and re-layouts  47.2 us
    another operation x36, local copies, waits for them, and re-layouts, closure_blocks(): stacked = jnp.stack(components, axis=0)  43.8 us
    all_gather x1, blocking collectives, shards(): every_means = lax.all_gather(own_means, ('gx', 'gy'), axis=0, tiled=False)  39.9 us
    convert_element_type x1, local copies, waits for them, and re-layouts, quantities(): tiles.astype(jnp.float32)  34.8 us
  transfers between devices with their start and end apart: 5, of which 2 were waited for; matrix products, arithmetic and copies ran while one was open for 11% of the time, Pallas kernels for 0%

profile of v3, /device:TPU:1, one launch (start us, length us, event | category | flops | bytes accessed | tf_op | source)
XLA Modules:
  0.0 621.3 jit_solution(15650472600734173896)
XLA Ops:
  9.0 15.6 %copy.123 = bf16[10,32,64,128]{2,1,3,0:T(8,128)(2,1)} copy(bf16[10,32,64,128]{3,2,1,0:T(8,128)(2,1)} %param.4) | data formatting | bytes 10485760 | tf_op args[0]
  57.2 8.7 %copy.122 = bf16[10,32,4,128]{2,1,3,0:T(8,128)(2,1)} copy(bf16[10,32,4,128]{3,1,2,0:T(8,128)(2,1)} %collective-permute-done) | data formatting | bytes 655360 | tf_op jit(solution)/shard_map/ppermute | solution.py:20
  65.8 8.8 %copy.124 = bf16[10,32,4,128]{2,1,3,0:T(8,128)(2,1)} copy(bf16[10,32,4,128]{3,1,2,0:T(8,128)(2,1)} %collective-permute-done.1) | data formatting | bytes 655360 | tf_op jit(solution)/shard_map/ppermute | solution.py:23
  86.0 65.8 %fusion = bf16[10,40,72,136]{2,1,3,0:T(8,128)(2,1)} fusion(bf16[10,32,72,4]{2,1,3,0:T(8,128)(2,1)S(1)} %collective-permute-done.3, bf16[10,32,72,4]{2,1,3,0:T(8,128)(2,1)S(1)} %collective-permute-done.2, bf16[10,32,4,128]{2,1,3,0:T(8,128)(2,1)S(1)} %copy-done.1, bf16[10,32,64,128]{2,1,3,0:T(8,128)(2,1)} %copy.123, bf16[10,32,4,128]{2,1,3,0:T(8,128)(2,1)S(1)} %bitcast.326), kind=kLoop, calls=%fused_computation.7 | loop fusion | flops 117504000 | bytes 14100480 | tf_op jit(solution)/shard_map/concatenate | solution.py:134
  151.8 151.1 %while.1 = (s32[]{:T(128)}, bf16[10,40,72,136]{2,1,3,0:T(8,128)(2,1)}, s32[20,4]{0,1:T(4,128)S(1)}, bf16[20,10,24,24,24]{4,3,2,1,0:T(8,128)(2,1)}, s32[]{:T(128)}) while((s32[]{:T(128)}, bf16[10,40,72,136]{2,1,3,0:T(8,128)(2,1)}, s32[20,4]{0,1:T(4,128)S(1)}, bf16[20,10,24,24,24]{4,3,2,1,0:T(8,128)(2,1)}, s32[]{:T(128)}) %tuple.64), condition=%wide.while_cond, body=%wide.while_body.sunk | while | flops 2 | bytes 2857605 | solution.py:114
  152.5 4.5 constant_dynamic-slice_fusion.8
  160.0 4.5 constant_dynamic-slice_fusion.8
  167.5 4.5 constant_dynamic-slice_fusion.8
  175.1 4.5 constant_dynamic-slice_fusion.8
  182.7 4.5 constant_dynamic-slice_fusion.8
  190.3 4.5 constant_dynamic-slice_fusion.8
  197.9 4.5 constant_dynamic-slice_fusion.8
  205.4 4.5 constant_dynamic-slice_fusion.8
  213.0 4.5 constant_dynamic-slice_fusion.8
  220.5 4.5 constant_dynamic-slice_fusion.8
  228.1 4.5 constant_dynamic-slice_fusion.8
  235.6 4.5 constant_dynamic-slice_fusion.8
  243.2 4.5 constant_dynamic-slice_fusion.8
  250.7 4.5 constant_dynamic-slice_fusion.8
  258.2 4.5 constant_dynamic-slice_fusion.8
  265.8 4.5 constant_dynamic-slice_fusion.8
  273.3 4.5 constant_dynamic-slice_fusion.8
  302.9 34.8 %reshape.794 = f32[20,10,24,576]{3,2,1,0:T(8,128)} reshape(bf16[20,10,24,24,24]{4,3,2,1,0:T(8,128)(2,1)} %get-tuple-element.9) | data formatting | bytes 16588800 | tf_op jit(solution)/shard_map/convert_element_type | solution.py:52
  348.3 15.9 %fusion.119 = f32[17,20,576,16]{2,3,1,0:T(8,128)} fusion(f32[17,20,24,576]{3,2,1,0:T(8,128)S(1)} %multiply_dynamic-update-slice_fusion), kind=kOutput, calls=%fused_computation.271 | convolution fusion | flops 902432640 | bytes 31334400 | tf_op jit(solution)/shard_map/az,qtzp->qtap/dot_general | solution.py:45
  364.2 16.5 %fusion.8 = f32[17,20,16,256]{3,2,1,0:T(8,128)S(1)} fusion(f32[17,20,576,16]{2,3,1,0:T(8,128)} %fusion.119, f32[576,256]{0,1:T(8,128)S(1)} %copy-done.5), kind=kOutput, calls=%fused_computation.22 | convolution fusion | flops 9625927680 | bytes 18694144 | tf_op jit(solution)/shard_map/qtap,pc->qtac/dot_general | solution.py:46
  382.5 15.5 %fusion.117 = f32[17,20,576,16]{2,3,1,0:T(8,128)} fusion(f32[17,20,24,576]{3,2,1,0:T(8,128)S(1)} %multiply_dynamic-update-slice_fusion), kind=kOutput, calls=%fused_computation.269 | convolution fusion | flops 902432640 | bytes 31334400 | tf_op jit(solution)/shard_map/az,qtzp->qtap/dot_general | solution.py:45
  398.0 16.7 %fusion.6 = f32[17,20,16,256]{3,2,1,0:T(8,128)S(1)} fusion(f32[17,20,576,16]{2,3,1,0:T(8,128)} %fusion.117, f32[576,256]{0,1:T(8,128)S(1)} %copy-done.4), kind=kOutput, calls=%fused_computation.20 | convolution fusion | flops 9625927680 | bytes 18694144 | tf_op jit(solution)/shard_map/qtap,pc->qtac/dot_general | solution.py:46
  417.3 15.5 %fusion.115 = f32[17,20,576,16]{2,3,1,0:T(8,128)} fusion(f32[17,20,24,576]{3,2,1,0:T(8,128)S(1)} %multiply_dynamic-update-slice_fusion), kind=kOutput, calls=%fused_computation.267 | convolution fusion | flops 902432640 | bytes 31334400 | tf_op jit(solution)/shard_map/az,qtzp->qtap/dot_general | solution.py:45
  432.8 16.7 %fusion.4 = f32[17,20,16,256]{3,2,1,0:T(8,128)S(1)} fusion(f32[17,20,576,16]{2,3,1,0:T(8,128)} %fusion.115, f32[576,256]{0,1:T(8,128)S(1)} %copy-done.3), kind=kOutput, calls=%fused_computation.18 | convolution fusion | flops 9625927680 | bytes 18694144 | tf_op jit(solution)/shard_map/qtap,pc->qtac/dot_general | solution.py:46
  452.1 15.5 %fusion.113 = f32[17,20,576,16]{2,3,1,0:T(8,128)} fusion(f32[17,20,24,576]{3,2,1,0:T(8,128)S(1)} %multiply_dynamic-update-slice_fusion), kind=kOutput, calls=%fused_computation.265 | convolution fusion | flops 902432640 | bytes 31334400 | tf_op jit(solution)/shard_map/az,qtzp->qtap/dot_general | solution.py:45
  467.6 16.9 %fusion.2 = f32[17,20,16,256]{3,2,1,0:T(8,128)S(1)} fusion(f32[17,20,576,16]{2,3,1,0:T(8,128)} %fusion.113, f32[576,256]{0,1:T(8,128)S(1)} %copy-done.2), kind=kOutput, calls=%fused_computation.16 | convolution fusion | flops 9625927680 | bytes 18694144 | tf_op jit(solution)/shard_map/qtap,pc->qtac/dot_general | solution.py:46
  572.6 39.9 %all_gather.4 = f32[128,20,32]{2,1,0:T(8,128)} all-gather(f32[1,20,32]{2,1,0:T(8,128)S(1)} %copy.145), channel_id=1, replica_groups=mesh['gx'=16,'gy'=8] {'gx','gy'}, dimensions={0}, use_global_device_ids=true | all-gather | bytes 330240 | tf_op jit(solution)/shard_map/all_gather | solution.py:177
  (315 shorter events, 240.9 us)
Async XLA Ops:
  2.3 54.8 %collective-permute-start = (bf16[10,32,4,128]{3,1,2,0:T(8,128)(2,1)S(1)}, bf16[10,32,4,128]{3,1,2,0:T(8,128)(2,1)}, u32[]{:S(2)}, u32[]{:S(2)}) collective-permute-start(bf16[10,32,4,128]{3,1,2,0:T(8,128)(2,1)S(1)} %copy.172), channel_id=1, source_target_pairs={{0,8},{8,16},{16,24},{24,32},{32,40},{40,48},{48,56},{56,64},{64,7... | collective-permute-start | bytes 983048 | tf_op jit(solution)/shard_map/ppermute | solution.py:20
  5.3 60.5 %collective-permute-start.1 = (bf16[10,32,4,128]{3,1,2,0:T(8,128)(2,1)}, bf16[10,32,4,128]{3,1,2,0:T(8,128)(2,1)}, u32[]{:S(2)}, u32[]{:S(2)}) collective-permute-start(bf16[10,32,4,128]{3,1,2,0:T(8,128)(2,1)} %copy.173), channel_id=1, source_target_pairs={{8,0},{16,8},{24,16},{32,24},{40,32},{48,40},{56,48},{64,56},{72,6... | collective-permute-start | bytes 983048 | tf_op jit(solution)/shard_map/ppermute | solution.py:23
  9.0 24.8 %copy-start.10 = (s32[8,16,20]{2,1,0:T(8,128)S(1)}, s32[8,16,20]{2,1,0:T(8,128)}, u32[]{:S(2)}) copy-start(s32[8,16,20]{2,1,0:T(8,128)} %param.5) | copy-start | bytes 30724
  65.8 20.1 %slice-start = ((s8[10485760]{0:T(1024)(128)(4,1)}), s8[2097152]{0:T(1024)(128)(4,1)S(1)}, s32[]{:S(2)}) async-start(s8[10485760]{0:T(1024)(128)(4,1)} %bitcast.325), calls=%async_computation.1 | async-start | bytes 4194304
  74.6 11.4 %slice-start.1 = ((s8[10485760]{0:T(1024)(128)(4,1)}), s8[4194304]{0:T(1024)(128)(4,1)S(1)}, s32[]{:S(2)}) async-start(s8[10485760]{0:T(1024)(128)(4,1)} %bitcast.325), calls=%async_computation.2 | async-start | bytes 8388608
  74.6 11.4 %slice-start.2 = ((s8[10485760]{0:T(1024)(128)(4,1)}), s8[4194304]{0:T(1024)(128)(4,1)S(1)}, s32[]{:S(2)}) async-start(s8[10485760]{0:T(1024)(128)(4,1)} %bitcast.325), calls=%async_computation.3 | async-start | bytes 8388608
  74.6 11.4 %copy-start.1 = (bf16[10,32,4,128]{2,1,3,0:T(8,128)(2,1)S(1)}, bf16[10,32,4,128]{2,1,3,0:T(8,128)(2,1)}, u32[]{:S(2)}) copy-start(bf16[10,32,4,128]{2,1,3,0:T(8,128)(2,1)} %copy.124) | copy-start | bytes 983044
  76.9 6.6 %collective-permute-start.2 = (bf16[10,32,72,4]{2,1,3,0:T(8,128)(2,1)S(1)}, bf16[10,32,72,4]{2,1,3,0:T(8,128)(2,1)S(1)}, u32[]{:S(2)}, u32[]{:S(2)}) collective-permute-start(bf16[10,32,72,4]{2,1,3,0:T(8,128)(2,1)S(1)} %get-tuple-element.45), channel_id=1, source_target_pairs={{0,1},{1,2},{2,3},{3,4},{4,5},{5,6},{6,7},{7,0},{8,9},{9,10},{10,1... | collective-permute-start | bytes 552968 | tf_op jit(solution)/shard_map/ppermute | solution.py:20
  79.5 6.5 %collective-permute-start.3 = (bf16[10,32,72,4]{2,1,3,0:T(8,128)(2,1)S(1)}, bf16[10,32,72,4]{2,1,3,0:T(8,128)(2,1)S(1)}, u32[]{:S(2)}, u32[]{:S(2)}) collective-permute-start(bf16[10,32,72,4]{2,1,3,0:T(8,128)(2,1)S(1)} %get-tuple-element.46), channel_id=1, source_target_pairs={{1,0},{2,1},{3,2},{4,3},{5,4},{6,5},{7,6},{0,7},{9,8},{10,9},{11,1... | collective-permute-start | bytes 552968 | tf_op jit(solution)/shard_map/ppermute | solution.py:23
  337.7 9.1 %copy-start = (f32[20,10,24,576]{3,2,1,0:T(8,128)S(1)}, f32[20,10,24,576]{3,2,1,0:T(8,128)}, u32[]{:S(2)}) copy-start(f32[20,10,24,576]{3,2,1,0:T(8,128)} %reshape.794) | copy-start | bytes 33177604
  348.3 15.9 %copy-start.5 = (f32[576,256]{0,1:T(8,128)S(1)}, f32[576,256]{0,1:T(8,128)}, u32[]{:S(2)}) copy-start(f32[576,256]{0,1:T(8,128)} %reshape.715) | copy-start | bytes 1769476
  382.5 15.5 %copy-start.4 = (f32[576,256]{0,1:T(8,128)S(1)}, f32[576,256]{0,1:T(8,128)}, u32[]{:S(2)}) copy-start(f32[576,256]{0,1:T(8,128)} %reshape.716) | copy-start | bytes 1769476
  417.3 15.5 %copy-start.3 = (f32[576,256]{0,1:T(8,128)S(1)}, f32[576,256]{0,1:T(8,128)}, u32[]{:S(2)}) copy-start(f32[576,256]{0,1:T(8,128)} %reshape.717) | copy-start | bytes 1769476
  452.1 15.5 %copy-start.2 = (f32[576,256]{0,1:T(8,128)S(1)}, f32[576,256]{0,1:T(8,128)}, u32[]{:S(2)}) copy-start(f32[576,256]{0,1:T(8,128)} %reshape.718) | copy-start | bytes 1769476
  492.5 12.9 %copy-start.12 = (s32[256]{0:T(256)S(1)}, s32[256]{0:T(256)}, u32[]{:S(2)}) copy-start(s32[256]{0:T(256)} %get-tuple-element.90) | copy-start | bytes 3076
  492.5 12.9 %copy-start.13 = (s32[256]{0:T(256)S(1)}, s32[256]{0:T(256)}, u32[]{:S(2)}) copy-start(s32[256]{0:T(256)} %get-tuple-element.91) | copy-start | bytes 3076
  492.5 12.9 %copy-start.14 = (s32[256]{0:T(256)S(1)}, s32[256]{0:T(256)}, u32[]{:S(2)}) copy-start(s32[256]{0:T(256)} %get-tuple-element.92) | copy-start | bytes 3076
  492.5 12.9 %copy-start.15 = (s32[256]{0:T(256)S(1)}, s32[256]{0:T(256)}, u32[]{:S(2)}) copy-start(s32[256]{0:T(256)} %get-tuple-element.93) | copy-start | bytes 3076
  492.6 12.9 %copy-start.16 = (pred[256]{0:T(512)(128)(4,1)S(1)}, pred[256]{0:T(512)(128)(4,1)}, u32[]{:S(2)}) copy-start(pred[256]{0:T(512)(128)(4,1)} %get-tuple-element.88) | copy-start | bytes 772
  492.6 12.9 %copy-start.17 = (pred[256]{0:T(512)(128)(4,1)S(1)}, pred[256]{0:T(512)(128)(4,1)}, u32[]{:S(2)}) copy-start(pred[256]{0:T(512)(128)(4,1)} %get-tuple-element.89) | copy-start | bytes 772
  506.4 9.8 %copy-start.8 = (f32[1,20,16,256]{3,2,1,0:T(8,128)S(1)}, f32[1,20,16,256]{3,2,1,0:T(8,128)}, u32[]{:S(2)}) copy-start(f32[1,20,16,256]{3,2,1,0:T(8,128)} %get-tuple-element.60) | copy-start | bytes 983044
  526.4 9.8 %copy-start.7 = (f32[1,20,16,256]{3,2,1,0:T(8,128)S(1)}, f32[1,20,16,256]{3,2,1,0:T(8,128)}, u32[]{:S(2)}) copy-start(f32[1,20,16,256]{3,2,1,0:T(8,128)} %get-tuple-element.68) | copy-start | bytes 983044
  546.4 9.8 %copy-start.6 = (f32[1,20,16,256]{3,2,1,0:T(8,128)S(1)}, f32[1,20,16,256]{3,2,1,0:T(8,128)}, u32[]{:S(2)}) copy-start(f32[1,20,16,256]{3,2,1,0:T(8,128)} %get-tuple-element.76) | copy-start | bytes 983044
  558.1 9.0 %copy-start.18 = (pred[20]{0:T(512)(128)(4,1)S(1)}, pred[20]{0:T(512)(128)(4,1)}, u32[]{:S(2)}) copy-start(pred[20]{0:T(512)(128)(4,1)} %get-tuple-element.38) | copy-start | bytes 64
  566.9 50.8 %copy-start.9 = (f32[2560,32]{0,1:T(8,128)S(1)}, f32[2560,32]{0,1:T(8,128)}, u32[]{:S(2)}) copy-start(f32[2560,32]{0,1:T(8,128)} %fusion.72) | copy-start | bytes 983044
  566.9 50.8 %copy-start.11 = (f32[2560,4]{0,1:T(4,128)S(1)}, f32[2560,4]{0,1:T(4,128)}, u32[]{:S(2)}) copy-start(f32[2560,4]{0,1:T(4,128)} %convert_bitcast_fusion) | copy-start | bytes 122884
  566.9 50.8 %copy-start.19 = (f32[4,32]{1,0:T(4,128)S(1)}, f32[4,32]{1,0:T(4,128)}, u32[]{:S(2)}) copy-start(f32[4,32]{1,0:T(4,128)} %convolution_maximum_fusion) | copy-start | bytes 1540
  569.1 50.5 %all-to-all-start = ((f32[16,2,2048]{2,1,0:T(2,128)}), f32[16,2,2048]{2,1,0:T(2,128)S(1)}, u32[]{:S(2)}, u32[]{:S(2)}) async-start(f32[16,2,2048]{2,1,0:T(2,128)} %reshape.720), calls=%async_computation | async-start | bytes 524288 | tf_op jit(solution)/shard_map/all_to_all | solution.py:170

commit v4 on v3

--- a/solution.py
+++ b/solution.py
@@ -109,16 +109,15 @@
     depth_at = tile_ids // (across_x * across_y)
     column_at = tile_ids // across_y % across_x
     row_at = tile_ids % across_y
-
-    def single_tile(depth_one, column_one, row_one):
-        return lax.dynamic_slice(
+    pieces = []
+    for index in range(tile_ids.shape[0]):
+        window = lax.dynamic_slice(
             padded,
-            (jnp.int32(0), depth_one * TE, column_one * TE, row_one * TE),
+            (jnp.int32(0), depth_at[index] * TE, column_at[index] * TE, row_at[index] * TE),
             (padded.shape[0], span, span, span),
         )
-
-    pieces = jax.vmap(single_tile)(depth_at, column_at, row_at)
-    return pieces.reshape(tile_ids.shape[0], padded.shape[0], span * span * span)
+        pieces.append(window.reshape(padded.shape[0], span * span * span))
+    return jnp.stack(pieces, axis=0)
 
 
 def shards(fields, dense_list, filter_device, pencil_order):

time: 634 us -> 613 us (0.967)
  between operations: 1.68 us -> 38 us
  local copies, waits for them, and re-layouts: 321 us -> 293 us
  other arithmetic: 106 us -> 78.2 us
    gather x100 -> x0, local copies, waits for them, and re-layouts: 151 us -> none
    dynamic_slice x0 -> x24, local copies, waits for them, and re-layouts: none -> 85.5 us  [cut_tiles(): lax.dynamic_slice(padded, (jnp.int32(0), depth_at[index] * TE, column_at[...]
    another operation x2 -> x22, local copies, waits for them, and re-layouts: 0.12 us -> 54 us  [the longest x21 53.9 us: cut_tiles(): return jnp.stack(pieces, axis=0)]
    convert_element_type x1 -> x0, local copies, waits for them, and re-layouts: 34.8 us -> none  [quantities(): tiles.astype(jnp.float32)]
    concatenate x1, other arithmetic: 65.8 us -> 34.7 us  [shards(): padded = jnp.concatenate([padded[:, -HW:], padded, padded[:, :HW]], axis=1)]
    unnamed x83 -> x120, local copies, waits for them, and re-layouts: 47.2 us -> 62.9 us
where the time goes in v4:
time: 613 us; the launch traced here: 601 us
  local copies, waits for them, and re-layouts  293 us (48%)
  matrix products  134 us (22%)
  other arithmetic  78.2 us (13%)
  blocking collectives  40 us (7%)
  between operations  38 us (6%)
  starting transfers between devices  12 us (2%)
    dynamic_slice x24, local copies, waits for them, and re-layouts, cut_tiles(): lax.dynamic_slice(padded, (jnp.int32(0), depth_at[index] * TE, column_at[...  85.5 us
    dot_general x4, matrix products, box_band(): jnp.einsum('qtap,pc->qtac', along_z, plane_matrix(half_width), precision=...  67 us
    unnamed x120, local copies, waits for them, and re-layouts  62.9 us
    dot_general x4, matrix products, box_band(): jnp.einsum('az,qtzp->qtap', band_matrix(half_width), columns, precision=H...  61.7 us
    another operation x21, local copies, waits for them, and re-layouts, cut_tiles(): return jnp.stack(pieces, axis=0)  53.9 us
    another operation x36, local copies, waits for them, and re-layouts, closure_blocks(): stacked = jnp.stack(components, axis=0)  43.8 us
    all_gather x1, blocking collectives, shards(): every_means = lax.all_gather(own_means, ('gx', 'gy'), axis=0, tiled=False)  40 us
    concatenate x1, other arithmetic, shards(): padded = jnp.concatenate([padded[:, -HW:], padded, padded[:, :HW]], axis=1)  34.7 us
  transfers between devices with their start and end apart: 5, of which 2 were waited for; matrix products, arithmetic and copies ran while one was open for 11% of the time, Pallas kernels for 0%

profile of v4, /device:TPU:1, one launch (start us, length us, event | category | flops | bytes accessed | tf_op | source)
XLA Modules:
  0.0 601.2 jit_solution(16498851280384639931)
XLA Ops:
  5.3 3.6 collective-permute-start.1
  15.3 15.6 %copy.183 = bf16[10,32,64,128]{2,1,3,0:T(8,128)(2,1)} copy(bf16[10,32,64,128]{3,2,1,0:T(8,128)(2,1)} %param.4) | data formatting | bytes 10485760 | tf_op args[0]
  88.7 3.4 scatter_custom_fusion.1
  95.5 8.6 %copy.182 = bf16[10,32,4,128]{2,1,3,0:T(8,128)(2,1)} copy(bf16[10,32,4,128]{3,1,2,0:T(8,128)(2,1)} %collective-permute-done) | data formatting | bytes 655360 | tf_op jit(solution)/shard_map/ppermute | solution.py:20
  104.1 8.7 %copy.184 = bf16[10,32,4,128]{2,1,3,0:T(8,128)(2,1)} copy(bf16[10,32,4,128]{3,1,2,0:T(8,128)(2,1)} %collective-permute-done.1) | data formatting | bytes 655360 | tf_op jit(solution)/shard_map/ppermute | solution.py:23
  118.1 3.4 collective-permute-done.2
  124.0 34.7 %fusion = bf16[10,40,72,136]{2,1,3,0:T(8,128)(2,1)S(1)} fusion(bf16[10,32,72,4]{2,1,3,0:T(8,128)(2,1)S(1)} %collective-permute-done.3, bf16[10,32,72,4]{2,1,3,0:T(8,128)(2,1)S(1)} %collective-permute-done.2, bf16[10,32,4,128]{2,1,3,0:T(8,128)(2,1)} %copy.184, bf16[10,32,64,128]{2,1,3,0:T(8,128)(2,1)} %copy.183, bf16[10,32,4,128]{2,1,3,0:T(8,128)(2,1)} %copy.182), kind=kLoop, calls=%fused_computation.4 | loop fusion | flops 117504000 | bytes 14100480 | tf_op jit(solution)/shard_map/concatenate | solution.py:133
  158.7 5.0 copy-done
  172.6 13.0 %constant_dynamic-slice_fusion.12 = (bf16[10,24,24,24]{2,1,3,0:T(8,128)(2,1)S(1)}, bf16[10,24,24,24]{2,1,3,0:T(8,128)(2,1)S(1)}, bf16[10,24,24,24]{2,1,3,0:T(8,1...) fusion(bf16[10,40,72,136]{2,1,3,0:T(8,128)(2,1)} %copy-done, ...), kind=kLoop, calls=%fused_computation.324 | loop fusion | bytes 3317832 | tf_op jit(solution)/shard_map/dynamic_slice | solution.py:114
  188.3 3.0 stack.170
  205.7 3.0 stack.173
  210.4 3.0 stack.174
  216.0 12.9 %constant_dynamic-slice_fusion.6 = (bf16[10,24,24,24]{2,1,3,0:T(8,128)(2,1)S(1)}, bf16[10,24,24,24]{2,1,3,0:T(8,128)(2,1)S(1)}, bf16[10,24,24,24]{2,1,3,0:T(8,12...) fusion(bf16[10,40,72,136]{2,1,3,0:T(8,128)(2,1)} %copy-done, ...), kind=kLoop, calls=%fused_computation.318 | loop fusion | bytes 3317832 | tf_op jit(solution)/shard_map/dynamic_slice | solution.py:114
  231.7 3.3 stack.176
  249.2 3.0 stack.179
  253.9 3.0 stack.180
  259.7 12.9 %constant_dynamic-slice_fusion = (bf16[10,24,24,24]{2,1,3,0:T(8,128)(2,1)S(1)}, bf16[10,24,24,24]{2,1,3,0:T(8,128)(2,1)S(1)}, bf16[10,24,24,24]{2,1,3,0:T(8,128)...) fusion(bf16[10,40,72,136]{2,1,3,0:T(8,128)(2,1)} %copy-done, ...), kind=kLoop, calls=%fused_computation.312 | loop fusion | bytes 3317832 | tf_op jit(solution)/shard_map/dynamic_slice | solution.py:114
  275.4 3.0 stack.182
  292.8 3.0 stack.185
  297.5 3.0 stack.186
  322.7 3.7 convert_element_type.23
  328.5 15.4 %fusion.119 = f32[17,20,576,16]{2,3,1,0:T(8,128)} fusion(f32[17,20,24,576]{3,2,1,0:T(8,128)S(1)} %multiply_dynamic-update-slice_fusion), kind=kOutput, calls=%fused_computation.288 | convolution fusion | flops 902432640 | bytes 31334400 | tf_op jit(solution)/shard_map/az,qtzp->qtap/dot_general | solution.py:45
  343.9 16.9 %fusion.8 = f32[17,20,16,256]{3,2,1,0:T(8,128)S(1)} fusion(f32[17,20,576,16]{2,3,1,0:T(8,128)} %fusion.119, f32[576,256]{0,1:T(8,128)S(1)} %copy-done.4), kind=kOutput, calls=%fused_computation.19 | convolution fusion | flops 9625927680 | bytes 18694144 | tf_op jit(solution)/shard_map/qtap,pc->qtac/dot_general | solution.py:46
  362.7 15.4 %fusion.117 = f32[17,20,576,16]{2,3,1,0:T(8,128)} fusion(f32[17,20,24,576]{3,2,1,0:T(8,128)S(1)} %multiply_dynamic-update-slice_fusion), kind=kOutput, calls=%fused_computation.286 | convolution fusion | flops 902432640 | bytes 31334400 | tf_op jit(solution)/shard_map/az,qtzp->qtap/dot_general | solution.py:45
  378.1 16.7 %fusion.6 = f32[17,20,16,256]{3,2,1,0:T(8,128)S(1)} fusion(f32[17,20,576,16]{2,3,1,0:T(8,128)} %fusion.117, f32[576,256]{0,1:T(8,128)S(1)} %copy-done.3), kind=kOutput, calls=%fused_computation.17 | convolution fusion | flops 9625927680 | bytes 18694144 | tf_op jit(solution)/shard_map/qtap,pc->qtac/dot_general | solution.py:46
  397.4 15.4 %fusion.115 = f32[17,20,576,16]{2,3,1,0:T(8,128)} fusion(f32[17,20,24,576]{3,2,1,0:T(8,128)S(1)} %multiply_dynamic-update-slice_fusion), kind=kOutput, calls=%fused_computation.284 | convolution fusion | flops 902432640 | bytes 31334400 | tf_op jit(solution)/shard_map/az,qtzp->qtap/dot_general | solution.py:45
  412.8 16.5 %fusion.4 = f32[17,20,16,256]{3,2,1,0:T(8,128)S(1)} fusion(f32[17,20,576,16]{2,3,1,0:T(8,128)} %fusion.115, f32[576,256]{0,1:T(8,128)S(1)} %copy-done.2), kind=kOutput, calls=%fused_computation.15 | convolution fusion | flops 9625927680 | bytes 18694144 | tf_op jit(solution)/shard_map/qtap,pc->qtac/dot_general | solution.py:46
  432.0 15.4 %fusion.113 = f32[17,20,576,16]{2,3,1,0:T(8,128)} fusion(f32[17,20,24,576]{3,2,1,0:T(8,128)S(1)} %multiply_dynamic-update-slice_fusion), kind=kOutput, calls=%fused_computation.282 | convolution fusion | flops 902432640 | bytes 31334400 | tf_op jit(solution)/shard_map/az,qtzp->qtap/dot_general | solution.py:45
  447.4 16.9 %fusion.2 = f32[17,20,16,256]{3,2,1,0:T(8,128)S(1)} fusion(f32[17,20,576,16]{2,3,1,0:T(8,128)} %fusion.113, f32[576,256]{0,1:T(8,128)S(1)} %copy-done.1), kind=kOutput, calls=%fused_computation.13 | convolution fusion | flops 9625927680 | bytes 18694144 | tf_op jit(solution)/shard_map/qtap,pc->qtac/dot_general | solution.py:46
  548.9 3.5 all-to-all-start
  552.4 40.0 %all_gather.4 = f32[128,20,32]{2,1,0:T(8,128)} all-gather(f32[1,20,32]{2,1,0:T(8,128)S(1)} %copy.223), channel_id=1, replica_groups=mesh['gx'=16,'gy'=8] {'gx','gy'}, dimensions={0}, use_global_device_ids=true | all-gather | bytes 330240 | tf_op jit(solution)/shard_map/all_gather | solution.py:176
  592.4 3.4 copy.225
  (296 shorter events, 234.9 us)
Async XLA Ops:
  2.3 93.1 %collective-permute-start = (bf16[10,32,4,128]{3,1,2,0:T(8,128)(2,1)S(1)}, bf16[10,32,4,128]{3,1,2,0:T(8,128)(2,1)}, u32[]{:S(2)}, u32[]{:S(2)}) collective-permute-start(bf16[10,32,4,128]{3,1,2,0:T(8,128)(2,1)S(1)} %copy.248), channel_id=1, source_target_pairs={{0,8},{8,16},{16,24},{24,32},{32,40},{40,48},{48,56},{56,64},{64,7... | collective-permute-start | bytes 983048 | tf_op jit(solution)/shard_map/ppermute | solution.py:20
  5.3 98.8 %collective-permute-start.1 = (bf16[10,32,4,128]{3,1,2,0:T(8,128)(2,1)}, bf16[10,32,4,128]{3,1,2,0:T(8,128)(2,1)}, u32[]{:S(2)}, u32[]{:S(2)}) collective-permute-start(bf16[10,32,4,128]{3,1,2,0:T(8,128)(2,1)} %copy.249), channel_id=1, source_target_pairs={{8,0},{16,8},{24,16},{32,24},{40,32},{48,40},{56,48},{64,56},{72,6... | collective-permute-start | bytes 983048 | tf_op jit(solution)/shard_map/ppermute | solution.py:23
  15.3 53.1 %copy-start.22 = (s32[8,16,20]{2,1,0:T(8,128)S(1)}, s32[8,16,20]{2,1,0:T(8,128)}, u32[]{:S(2)}) copy-start(s32[8,16,20]{2,1,0:T(8,128)} %param.5) | copy-start | bytes 30724
  114.9 6.6 %collective-permute-start.2 = (bf16[10,32,72,4]{2,1,3,0:T(8,128)(2,1)S(1)}, bf16[10,32,72,4]{2,1,3,0:T(8,128)(2,1)S(1)}, u32[]{:S(2)}, u32[]{:S(2)}) collective-permute-start(bf16[10,32,72,4]{2,1,3,0:T(8,128)(2,1)S(1)} %get-tuple-element.6), channel_id=1, source_target_pairs={{0,1},{1,2},{2,3},{3,4},{4,5},{5,6},{6,7},{7,0},{8,9},{9,10},{10,1... | collective-permute-start | bytes 552968 | tf_op jit(solution)/shard_map/ppermute | solution.py:20
  117.5 6.5 %collective-permute-start.3 = (bf16[10,32,72,4]{2,1,3,0:T(8,128)(2,1)S(1)}, bf16[10,32,72,4]{2,1,3,0:T(8,128)(2,1)S(1)}, u32[]{:S(2)}, u32[]{:S(2)}) collective-permute-start(bf16[10,32,72,4]{2,1,3,0:T(8,128)(2,1)S(1)} %get-tuple-element.7), channel_id=1, source_target_pairs={{1,0},{2,1},{3,2},{4,3},{5,4},{6,5},{7,6},{0,7},{9,8},{10,9},{11,1... | collective-permute-start | bytes 552968 | tf_op jit(solution)/shard_map/ppermute | solution.py:23
  301.5 11.3 %copy-start.8 = (bf16[1,10,24,576]{3,2,0,1:T(8,128)(2,1)S(1)}, bf16[1,10,24,576]{3,2,0,1:T(8,128)(2,1)}, u32[]{:S(2)}) copy-start(bf16[1,10,24,576]{3,2,0,1:T(8,128)(2,1)} %stack.175) | copy-start | bytes 829444
  301.5 12.0 %copy-start.9 = (bf16[1,10,24,576]{3,2,0,1:T(8,128)(2,1)S(1)}, bf16[1,10,24,576]{3,2,0,1:T(8,128)(2,1)}, u32[]{:S(2)}) copy-start(bf16[1,10,24,576]{3,2,0,1:T(8,128)(2,1)} %stack.176) | copy-start | bytes 829444
  301.5 12.8 %copy-start.10 = (bf16[1,10,24,576]{3,2,0,1:T(8,128)(2,1)S(1)}, bf16[1,10,24,576]{3,2,0,1:T(8,128)(2,1)}, u32[]{:S(2)}) copy-start(bf16[1,10,24,576]{3,2,0,1:T(8,128)(2,1)} %stack.177) | copy-start | bytes 829444
  301.5 13.6 %copy-start.11 = (bf16[1,10,24,576]{3,2,0,1:T(8,128)(2,1)S(1)}, bf16[1,10,24,576]{3,2,0,1:T(8,128)(2,1)}, u32[]{:S(2)}) copy-start(bf16[1,10,24,576]{3,2,0,1:T(8,128)(2,1)} %stack.178) | copy-start | bytes 829444
  303.2 12.6 %copy-start.12 = (bf16[1,10,24,576]{3,2,0,1:T(8,128)(2,1)S(1)}, bf16[1,10,24,576]{3,2,0,1:T(8,128)(2,1)}, u32[]{:S(2)}) copy-start(bf16[1,10,24,576]{3,2,0,1:T(8,128)(2,1)} %stack.179) | copy-start | bytes 829444
  303.2 13.3 %copy-start.13 = (bf16[1,10,24,576]{3,2,0,1:T(8,128)(2,1)S(1)}, bf16[1,10,24,576]{3,2,0,1:T(8,128)(2,1)}, u32[]{:S(2)}) copy-start(bf16[1,10,24,576]{3,2,0,1:T(8,128)(2,1)} %stack.180) | copy-start | bytes 829444
  303.2 14.1 %copy-start.14 = (bf16[1,10,24,576]{3,2,0,1:T(8,128)(2,1)S(1)}, bf16[1,10,24,576]{3,2,0,1:T(8,128)(2,1)}, u32[]{:S(2)}) copy-start(bf16[1,10,24,576]{3,2,0,1:T(8,128)(2,1)} %stack.181) | copy-start | bytes 829444
  303.2 14.9 %copy-start.15 = (bf16[1,10,24,576]{3,2,0,1:T(8,128)(2,1)S(1)}, bf16[1,10,24,576]{3,2,0,1:T(8,128)(2,1)}, u32[]{:S(2)}) copy-start(bf16[1,10,24,576]{3,2,0,1:T(8,128)(2,1)} %stack.182) | copy-start | bytes 829444
  303.2 15.6 %copy-start.16 = (bf16[1,10,24,576]{3,2,0,1:T(8,128)(2,1)S(1)}, bf16[1,10,24,576]{3,2,0,1:T(8,128)(2,1)}, u32[]{:S(2)}) copy-start(bf16[1,10,24,576]{3,2,0,1:T(8,128)(2,1)} %stack.183) | copy-start | bytes 829444
  303.3 16.4 %copy-start.17 = (bf16[1,10,24,576]{3,2,0,1:T(8,128)(2,1)S(1)}, bf16[1,10,24,576]{3,2,0,1:T(8,128)(2,1)}, u32[]{:S(2)}) copy-start(bf16[1,10,24,576]{3,2,0,1:T(8,128)(2,1)} %stack.184) | copy-start | bytes 829444
  303.3 17.1 %copy-start.18 = (bf16[1,10,24,576]{3,2,0,1:T(8,128)(2,1)S(1)}, bf16[1,10,24,576]{3,2,0,1:T(8,128)(2,1)}, u32[]{:S(2)}) copy-start(bf16[1,10,24,576]{3,2,0,1:T(8,128)(2,1)} %stack.185) | copy-start | bytes 829444
  303.3 17.9 %copy-start.19 = (bf16[1,10,24,576]{3,2,0,1:T(8,128)(2,1)S(1)}, bf16[1,10,24,576]{3,2,0,1:T(8,128)(2,1)}, u32[]{:S(2)}) copy-start(bf16[1,10,24,576]{3,2,0,1:T(8,128)(2,1)} %stack.186) | copy-start | bytes 829444
  303.3 18.6 %copy-start.20 = (bf16[1,10,24,576]{3,2,0,1:T(8,128)(2,1)S(1)}, bf16[1,10,24,576]{3,2,0,1:T(8,128)(2,1)}, u32[]{:S(2)}) copy-start(bf16[1,10,24,576]{3,2,0,1:T(8,128)(2,1)} %stack.187) | copy-start | bytes 829444
  328.5 15.4 %copy-start.4 = (f32[576,256]{0,1:T(8,128)S(1)}, f32[576,256]{0,1:T(8,128)}, u32[]{:S(2)}) copy-start(f32[576,256]{0,1:T(8,128)} %reshape.678) | copy-start | bytes 1769476
  362.7 15.4 %copy-start.3 = (f32[576,256]{0,1:T(8,128)S(1)}, f32[576,256]{0,1:T(8,128)}, u32[]{:S(2)}) copy-start(f32[576,256]{0,1:T(8,128)} %reshape.679) | copy-start | bytes 1769476
  397.4 15.4 %copy-start.2 = (f32[576,256]{0,1:T(8,128)S(1)}, f32[576,256]{0,1:T(8,128)}, u32[]{:S(2)}) copy-start(f32[576,256]{0,1:T(8,128)} %reshape.680) | copy-start | bytes 1769476
  432.0 15.4 %copy-start.1 = (f32[576,256]{0,1:T(8,128)S(1)}, f32[576,256]{0,1:T(8,128)}, u32[]{:S(2)}) copy-start(f32[576,256]{0,1:T(8,128)} %reshape.681) | copy-start | bytes 1769476
  472.4 12.9 %copy-start.24 = (s32[256]{0:T(256)S(1)}, s32[256]{0:T(256)}, u32[]{:S(2)}) copy-start(s32[256]{0:T(256)} %get-tuple-element.127) | copy-start | bytes 3076
  472.4 12.9 %copy-start.25 = (s32[256]{0:T(256)S(1)}, s32[256]{0:T(256)}, u32[]{:S(2)}) copy-start(s32[256]{0:T(256)} %get-tuple-element.128) | copy-start | bytes 3076
  472.4 12.9 %copy-start.26 = (s32[256]{0:T(256)S(1)}, s32[256]{0:T(256)}, u32[]{:S(2)}) copy-start(s32[256]{0:T(256)} %get-tuple-element.129) | copy-start | bytes 3076
  472.4 12.9 %copy-start.27 = (s32[256]{0:T(256)S(1)}, s32[256]{0:T(256)}, u32[]{:S(2)}) copy-start(s32[256]{0:T(256)} %get-tuple-element.130) | copy-start | bytes 3076
  472.4 12.9 %copy-start.28 = (pred[256]{0:T(512)(128)(4,1)S(1)}, pred[256]{0:T(512)(128)(4,1)}, u32[]{:S(2)}) copy-start(pred[256]{0:T(512)(128)(4,1)} %get-tuple-element.125) | copy-start | bytes 772
  472.4 12.9 %copy-start.29 = (pred[256]{0:T(512)(128)(4,1)S(1)}, pred[256]{0:T(512)(128)(4,1)}, u32[]{:S(2)}) copy-start(pred[256]{0:T(512)(128)(4,1)} %get-tuple-element.126) | copy-start | bytes 772
  546.7 50.9 %copy-start.21 = (f32[2560,32]{0,1:T(8,128)S(1)}, f32[2560,32]{0,1:T(8,128)}, u32[]{:S(2)}) copy-start(f32[2560,32]{0,1:T(8,128)} %fusion.72) | copy-start | bytes 983044
  546.7 50.9 %copy-start.23 = (f32[2560,4]{0,1:T(4,128)S(1)}, f32[2560,4]{0,1:T(4,128)}, u32[]{:S(2)}) copy-start(f32[2560,4]{0,1:T(4,128)} %convert_bitcast_fusion) | copy-start | bytes 122884
  546.7 50.9 %copy-start.31 = (f32[4,32]{1,0:T(4,128)S(1)}, f32[4,32]{1,0:T(4,128)}, u32[]{:S(2)}) copy-start(f32[4,32]{1,0:T(4,128)} %convolution_maximum_fusion) | copy-start | bytes 1540
  548.9 50.6 %all-to-all-start = ((f32[16,2,2048]{2,1,0:T(2,128)}), f32[16,2,2048]{2,1,0:T(2,128)S(1)}, u32[]{:S(2)}, u32[]{:S(2)}) async-start(f32[16,2,2048]{2,1,0:T(2,128)} %reshape.683), calls=%async_computation | async-start | bytes 524288 | tf_op jit(solution)/shard_map/all_to_all | solution.py:169
  (5 other events, 43.3 us)

commit v5 on v4

--- a/solution.py
+++ b/solution.py
@@ -1,3 +1,4 @@
+import numpy as np
 import jax
 import jax.numpy as jnp
 from jax import lax
@@ -27,18 +28,16 @@
 
 def band_matrix(half_width):
     span = TE + 2 * HW
-    row_index = lax.broadcasted_iota(jnp.int32, (TE, span), 0)
-    column_index = lax.broadcasted_iota(jnp.int32, (TE, span), 1)
-    inside = jnp.abs(column_index - row_index - HW) <= half_width
-    return jnp.where(inside, 1.0 / (2 * half_width + 1), 0.0).astype(jnp.float32)
+    row_index = np.arange(TE)[:, None]
+    column_index = np.arange(span)[None, :]
+    inside = np.abs(column_index - row_index - HW) <= half_width
+    return np.where(inside, np.float32(1.0 / (2 * half_width + 1)), np.float32(0.0)).astype(np.float32)
 
 
 def plane_matrix(half_width):
     span = TE + 2 * HW
-    weights = band_matrix(half_width)
-    return jnp.einsum("ax,by->xyab", weights, weights, precision=HIGHEST).reshape(
-        span * span, TE * TE
-    )
+    weights = band_matrix(half_width).astype(np.float64)
+    return np.einsum("ax,by->xyab", weights, weights).reshape(span * span, TE * TE).astype(np.float32)
 
 
 def box_band(columns, half_width):
@@ -68,10 +67,10 @@
 
 def block_matrix():
     sub_edge = TE // 4
-    plane_index = lax.broadcasted_iota(jnp.int32, (TE * TE, sub_edge * sub_edge), 0)
-    block_index = lax.broadcasted_iota(jnp.int32, (TE * TE, sub_edge * sub_edge), 1)
+    plane_index = np.arange(TE * TE)[:, None]
+    block_index = np.arange(sub_edge * sub_edge)[None, :]
     block_of = plane_index // TE // 4 * sub_edge + plane_index % TE // 4
-    return jnp.where(block_of == block_index, 1.0 / 16.0, 0.0).astype(jnp.float32)
+    return np.where(block_of == block_index, np.float32(1.0 / 16.0), np.float32(0.0)).astype(np.float32)
 
 
 def closure_blocks(smoothed):
@@ -87,9 +86,14 @@
     components.append(smoothed[12] / solid_mean)
     components.append(smoothed[13] / solid_mean - smoothed[4])
     sub_edge = TE // 4
-    stacked = jnp.stack(components, axis=0)
-    tile_count = stacked.shape[1]
-    depth_mean = jnp.mean(stacked.reshape(8, tile_count, sub_edge, 4, TE * TE), axis=3)
+    tile_count = components[0].shape[0]
+    depth_mean = jnp.stack(
+        [
+            jnp.mean(component.reshape(tile_count, sub_edge, 4, TE * TE), axis=2)
+            for component in components
+        ],
+        axis=0,
+    )
     blocks = jnp.einsum("ktzp,pc->ktzc", depth_mean, block_matrix(), precision=HIGHEST)
     return blocks.reshape(8, tile_count, sub_edge**3)
 

time: 613 us -> 589 us (0.961)
  other arithmetic: 78.2 us -> 66.9 us
  local copies, waits for them, and re-layouts: 293 us -> 283 us
    squeeze x0 -> x68, local copies, waits for them, and re-layouts: none -> 60.8 us  [the longest x12 21.5 us: closure_blocks(): smoothed[9 + direction]]
    another operation x37 -> x1, local copies, waits for them, and re-layouts: 43.9 us -> 0.12 us  [the longest x36 43.8 us: closure_blocks(): stacked = jnp.stack(components, axis=0)]
    unnamed x120 -> x86, local copies, waits for them, and re-layouts: 62.9 us -> 41.8 us
    reduce_sum x4, other arithmetic: 8.21 us -> 17.4 us  [closure_blocks(): jnp.mean(component.reshape(tile_count, sub_edge, 4, TE * TE), axis=2)]
    dot_general x4, matrix products: 67 us -> 59.6 us  [box_band(): jnp.einsum('qtap,pc->qtac', along_z, plane_matrix(half_width), precision=...]
    slice x1 -> x5, local copies, waits for them, and re-layouts: 0.07 us -> 7.18 us  [the longest x4 7.1 us: closure_blocks(): smoothed[9 + direction]]
    reshape x5 -> x1, local copies, waits for them, and re-layouts: 7.1 us -> 0.01 us  [the longest x4 7.1 us: plane_matrix(): jnp.einsum('ax,by->xyab', weights, weights, precision=HIGHEST)]
    sub x4 -> x0, other arithmetic: 6.18 us -> none  [closure_blocks(): components.append(smoothed[13] / solid_mean - smoothed[4])]
  transfers between devices with their start and end apart: 5 -> 5, of which waited for: 2 -> 2; matrix products, arithmetic and copies ran while one was open for 11% -> 8% of each run, Pallas kernels for 0% -> 0%
where the time goes in v5:
time: 589 us; the launch traced here: 581 us
  local copies, waits for them, and re-layouts  283 us (48%)
  matrix products  136 us (23%)
  other arithmetic  66.9 us (11%)
  blocking collectives  40.1 us (7%)
  between operations  38.1 us (6%)
  starting transfers between devices  12 us (2%)
  waiting for transfers between devices  5.92 us (1%)
    dynamic_slice x24, local copies, waits for them, and re-layouts, cut_tiles(): lax.dynamic_slice(padded, (jnp.int32(0), depth_at[index] * TE, column_at[...  85.3 us
    dot_general x4, matrix products, box_band(): jnp.einsum('az,qtzp->qtap', band_matrix(half_width), columns, precision=H...  65.8 us
    dot_general x4, matrix products, box_band(): jnp.einsum('qtap,pc->qtac', along_z, plane_matrix(half_width), precision=...  59.6 us
    another operation x21, local copies, waits for them, and re-layouts, cut_tiles(): return jnp.stack(pieces, axis=0)  53.8 us
    unnamed x86, local copies, waits for them, and re-layouts  41.8 us
    all_gather x1, blocking collectives, shards(): every_means = lax.all_gather(own_means, ('gx', 'gy'), axis=0, tiled=False)  40.1 us
    concatenate x1, other arithmetic, shards(): padded = jnp.concatenate([padded[:, -HW:], padded, padded[:, :HW]], axis=1)  34.7 us
    squeeze x12, local copies, waits for them, and re-layouts, closure_blocks(): smoothed[9 + direction]  21.5 us
  transfers between devices with their start and end apart: 5, of which 2 were waited for; matrix products, arithmetic and copies ran while one was open for 8% of the time, Pallas kernels for 0%

profile of v5, /device:TPU:1, one launch (start us, length us, event | category | flops | bytes accessed | tf_op | source)
XLA Modules:
  0.0 581.4 jit_solution(1938888419261374094)
XLA Ops:
  4.6 3.7 collective-permute-start.1
  14.4 15.6 %copy.287 = bf16[10,32,64,128]{2,1,3,0:T(8,128)(2,1)} copy(bf16[10,32,64,128]{3,2,1,0:T(8,128)(2,1)} %param.16) | data formatting | bytes 10485760 | tf_op args[0]
  67.5 3.4 scatter_custom_fusion.1
  73.5 7.9 %copy.286 = bf16[10,32,4,128]{2,1,3,0:T(8,128)(2,1)} copy(bf16[10,32,4,128]{3,1,2,0:T(8,128)(2,1)S(1)} %collective-permute-done) | data formatting | bytes 655360 | tf_op jit(solution)/shard_map/ppermute | solution.py:21
  81.4 7.8 %copy.288 = bf16[10,32,4,128]{2,1,3,0:T(8,128)(2,1)} copy(bf16[10,32,4,128]{3,1,2,0:T(8,128)(2,1)S(1)} %collective-permute-done.1) | data formatting | bytes 655360 | tf_op jit(solution)/shard_map/ppermute | solution.py:24
  94.5 3.4 collective-permute-done.2
  100.4 34.7 %fusion = bf16[10,40,72,136]{2,1,3,0:T(8,128)(2,1)S(1)} fusion(bf16[10,32,72,4]{2,1,3,0:T(8,128)(2,1)S(1)} %collective-permute-done.3, bf16[10,32,72,4]{2,1,3,0:T(8,128)(2,1)S(1)} %collective-permute-done.2, bf16[10,32,4,128]{2,1,3,0:T(8,128)(2,1)} %copy.288, bf16[10,32,64,128]{2,1,3,0:T(8,128)(2,1)} %copy.287, bf16[10,32,4,128]{2,1,3,0:T(8,128)(2,1)} %copy.286), kind=kLoop, calls=%fused_computation.4 | loop fusion | flops 117504000 | bytes 14100480 | tf_op jit(solution)/shard_map/concatenate | solution.py:137
  135.1 5.0 copy-done.1
  149.1 12.7 %constant_dynamic-slice_fusion.12 = (bf16[10,24,24,24]{2,1,3,0:T(8,128)(2,1)S(1)}, bf16[10,24,24,24]{2,1,3,0:T(8,128)(2,1)S(1)}, bf16[10,24,24,24]{2,1,3,0:T(8,1...) fusion(bf16[10,40,72,136]{2,1,3,0:T(8,128)(2,1)} %copy-done.1, ...), kind=kLoop, calls=%fused_computation.236 | loop fusion | bytes 3317832 | tf_op jit(solution)/shard_map/dynamic_slice | solution.py:118
  186.5 3.0 stack.110
  192.1 13.1 %constant_dynamic-slice_fusion.6 = (bf16[10,24,24,24]{2,1,3,0:T(8,128)(2,1)S(1)}, bf16[10,24,24,24]{2,1,3,0:T(8,128)(2,1)S(1)}, bf16[10,24,24,24]{2,1,3,0:T(8,12...) fusion(bf16[10,40,72,136]{2,1,3,0:T(8,128)(2,1)} %copy-done.1, ...), kind=kLoop, calls=%fused_computation.230 | loop fusion | bytes 3317832 | tf_op jit(solution)/shard_map/dynamic_slice | solution.py:118
  207.9 3.3 stack.112
  230.1 3.0 stack.116
  235.9 13.1 %constant_dynamic-slice_fusion = (bf16[10,24,24,24]{2,1,3,0:T(8,128)(2,1)S(1)}, bf16[10,24,24,24]{2,1,3,0:T(8,128)(2,1)S(1)}, bf16[10,24,24,24]{2,1,3,0:T(8,128)...) fusion(bf16[10,40,72,136]{2,1,3,0:T(8,128)(2,1)} %copy-done.1, ...), kind=kLoop, calls=%fused_computation.224 | loop fusion | bytes 3317832 | tf_op jit(solution)/shard_map/dynamic_slice | solution.py:118
  257.5 3.0 stack.119
  269.0 3.0 stack.121
  299.7 3.7 convert_element_type.23
  305.9 15.3 %fusion.62 = f32[17,20,576,16]{2,3,1,0:T(8,128)} fusion(f32[17,20,24,576]{3,2,1,0:T(8,128)S(1)} %multiply_dynamic-update-slice_fusion, f32[16,24,1,1]{1,0,3,2:T(8,128)S(1)} %copy-done.25), kind=kOutput, calls=%fused_computation.284 | convolution fusion | flops 902430720 | bytes 31335936 | tf_op jit(solution)/shard_map/az,qtzp->qtap/dot_general | solution.py:44
  321.2 16.4 %fusion.8 = f32[17,20,16,256]{3,2,1,0:T(8,128)S(1)} fusion(f32[576,256,1,1]{1,0,3,2:T(8,128)S(1)} %copy-done.17, f32[17,20,576,16]{2,3,1,0:T(8,128)} %fusion.62), kind=kOutput, calls=%fused_computation.19 | convolution fusion | flops 9625927680 | bytes 18694144 | tf_op jit(solution)/shard_map/qtap,pc->qtac/dot_general | solution.py:45
  354.7 4.3 subtract_reduce_fusion.21
  361.5 16.8 %fusion.64 = f32[17,20,576,16]{2,3,1,0:T(8,128)S(1)} fusion(f32[17,20,24,576]{3,2,1,0:T(8,128)} %copy-done, f32[16,24,1,1]{1,0,3,2:T(8,128)S(1)} %copy-done.24), kind=kOutput, calls=%fused_computation.286 | convolution fusion | flops 902430720 | bytes 31335936 | tf_op jit(solution)/shard_map/az,qtzp->qtap/dot_general | solution.py:44
  378.3 14.4 %fusion.6 = f32[17,20,16,256]{3,2,1,0:T(8,128)S(1)} fusion(f32[576,256,1,1]{1,0,3,2:T(8,128)S(1)} %copy-done.16, f32[17,20,576,16]{2,3,1,0:T(8,128)S(1)} %fusion.64), kind=kOutput, calls=%fused_computation.17 | convolution fusion | flops 9625927680 | bytes 18694144 | tf_op jit(solution)/shard_map/qtap,pc->qtac/dot_general | solution.py:45
  409.7 4.3 subtract_reduce_fusion.14
  416.4 16.7 %fusion.66 = f32[17,20,576,16]{2,3,1,0:T(8,128)S(1)} fusion(f32[17,20,24,576]{3,2,1,0:T(8,128)} %copy-done, f32[16,24,1,1]{1,0,3,2:T(8,128)S(1)} %copy-done.23), kind=kOutput, calls=%fused_computation.288 | convolution fusion | flops 902430720 | bytes 31335936 | tf_op jit(solution)/shard_map/az,qtzp->qtap/dot_general | solution.py:44
  433.1 14.4 %fusion.4 = f32[17,20,16,256]{3,2,1,0:T(8,128)S(1)} fusion(f32[576,256,1,1]{1,0,3,2:T(8,128)S(1)} %copy-done.15, f32[17,20,576,16]{2,3,1,0:T(8,128)S(1)} %fusion.66), kind=kOutput, calls=%fused_computation.15 | convolution fusion | flops 9625927680 | bytes 18694144 | tf_op jit(solution)/shard_map/qtap,pc->qtac/dot_general | solution.py:45
  464.6 4.3 subtract_reduce_fusion.7
  471.3 17.1 %fusion.68 = f32[17,20,576,16]{2,3,1,0:T(8,128)S(1)} fusion(f32[17,20,24,576]{3,2,1,0:T(8,128)} %copy-done, f32[16,24,1,1]{1,0,3,2:T(8,128)S(1)} %copy-done.22), kind=kOutput, calls=%fused_computation.290 | convolution fusion | flops 902430720 | bytes 31335936 | tf_op jit(solution)/shard_map/az,qtzp->qtap/dot_general | solution.py:44
  488.4 14.3 %fusion.2 = f32[17,20,16,256]{3,2,1,0:T(8,128)S(1)} fusion(f32[576,256,1,1]{1,0,3,2:T(8,128)S(1)} %copy-done.14, f32[17,20,576,16]{2,3,1,0:T(8,128)S(1)} %fusion.68), kind=kOutput, calls=%fused_computation.13 | convolution fusion | flops 9625927680 | bytes 18694144 | tf_op jit(solution)/shard_map/qtap,pc->qtac/dot_general | solution.py:45
  519.8 4.3 subtract_reduce_fusion
  528.9 3.5 all-to-all-start
  532.5 40.1 %all_gather.4 = f32[128,20,32]{2,1,0:T(8,128)} all-gather(f32[1,20,32]{2,1,0:T(8,128)S(1)} %copy.347), channel_id=1, replica_groups=mesh['gx'=16,'gy'=8] {'gx','gy'}, dimensions={0}, use_global_device_ids=true | all-gather | bytes 330240 | tf_op jit(solution)/shard_map/all_gather | solution.py:180
  572.6 3.4 copy.349
  (303 shorter events, 214.0 us)
Async XLA Ops:
  2.3 71.2 %collective-permute-start = (bf16[10,32,4,128]{3,1,2,0:T(8,128)(2,1)S(1)}, bf16[10,32,4,128]{3,1,2,0:T(8,128)(2,1)S(1)}, u32[]{:S(2)}, u32[]{:S(2)}) collective-permute-start(bf16[10,32,4,128]{3,1,2,0:T(8,128)(2,1)S(1)} %copy.360), channel_id=1, source_target_pairs={{0,8},{8,16},{16,24},{24,32},{32,40},{40,48},{48,56},{56,64},{64,7... | collective-permute-start | bytes 983048 | tf_op jit(solution)/shard_map/ppermute | solution.py:21
  4.6 76.9 %collective-permute-start.1 = (bf16[10,32,4,128]{3,1,2,0:T(8,128)(2,1)S(1)}, bf16[10,32,4,128]{3,1,2,0:T(8,128)(2,1)S(1)}, u32[]{:S(2)}, u32[]{:S(2)}) collective-permute-start(bf16[10,32,4,128]{3,1,2,0:T(8,128)(2,1)S(1)} %copy.361), channel_id=1, source_target_pairs={{8,0},{16,8},{24,16},{32,24},{40,32},{48,40},{56,48},{64,56},{72,6... | collective-permute-start | bytes 983048 | tf_op jit(solution)/shard_map/ppermute | solution.py:24
  14.4 49.3 %copy-start.20 = (s32[8,16,20]{2,1,0:T(8,128)S(1)}, s32[8,16,20]{2,1,0:T(8,128)}, u32[]{:S(2)}) copy-start(s32[8,16,20]{2,1,0:T(8,128)} %param.17) | copy-start | bytes 30724
  14.4 56.9 %copy-start.27 = (s32[32]{0:T(128)S(1)}, s32[32]{0:T(128)}, u32[]{:S(2)}) copy-start(s32[32]{0:T(128)} %param.19) | copy-start | bytes 388
  91.3 6.6 %collective-permute-start.2 = (bf16[10,32,72,4]{2,1,3,0:T(8,128)(2,1)S(1)}, bf16[10,32,72,4]{2,1,3,0:T(8,128)(2,1)S(1)}, u32[]{:S(2)}, u32[]{:S(2)}) collective-permute-start(bf16[10,32,72,4]{2,1,3,0:T(8,128)(2,1)S(1)} %get-tuple-element.62), channel_id=1, source_target_pairs={{0,1},{1,2},{2,3},{3,4},{4,5},{5,6},{6,7},{7,0},{8,9},{9,10},{10,1... | collective-permute-start | bytes 552968 | tf_op jit(solution)/shard_map/ppermute | solution.py:21
  93.9 6.5 %collective-permute-start.3 = (bf16[10,32,72,4]{2,1,3,0:T(8,128)(2,1)S(1)}, bf16[10,32,72,4]{2,1,3,0:T(8,128)(2,1)S(1)}, u32[]{:S(2)}, u32[]{:S(2)}) collective-permute-start(bf16[10,32,72,4]{2,1,3,0:T(8,128)(2,1)S(1)} %get-tuple-element.63), channel_id=1, source_target_pairs={{1,0},{2,1},{3,2},{4,3},{5,4},{6,5},{7,6},{0,7},{9,8},{10,9},{11,1... | collective-permute-start | bytes 552968 | tf_op jit(solution)/shard_map/ppermute | solution.py:24
  277.7 12.9 %copy-start.2 = (bf16[1,10,24,576]{3,2,0,1:T(8,128)(2,1)S(1)}, bf16[1,10,24,576]{3,2,0,1:T(8,128)(2,1)}, u32[]{:S(2)}) copy-start(bf16[1,10,24,576]{3,2,0,1:T(8,128)(2,1)} %stack.112) | copy-start | bytes 829444
  277.7 13.6 %copy-start.3 = (bf16[1,10,24,576]{3,2,0,1:T(8,128)(2,1)S(1)}, bf16[1,10,24,576]{3,2,0,1:T(8,128)(2,1)}, u32[]{:S(2)}) copy-start(bf16[1,10,24,576]{3,2,0,1:T(8,128)(2,1)} %stack.113) | copy-start | bytes 829444
  277.7 14.4 %copy-start.4 = (bf16[1,10,24,576]{3,2,0,1:T(8,128)(2,1)S(1)}, bf16[1,10,24,576]{3,2,0,1:T(8,128)(2,1)}, u32[]{:S(2)}) copy-start(bf16[1,10,24,576]{3,2,0,1:T(8,128)(2,1)} %stack.114) | copy-start | bytes 829444
  277.7 15.1 %copy-start.5 = (bf16[1,10,24,576]{3,2,0,1:T(8,128)(2,1)S(1)}, bf16[1,10,24,576]{3,2,0,1:T(8,128)(2,1)}, u32[]{:S(2)}) copy-start(bf16[1,10,24,576]{3,2,0,1:T(8,128)(2,1)} %stack.115) | copy-start | bytes 829444
  279.4 14.2 %copy-start.6 = (bf16[1,10,24,576]{3,2,0,1:T(8,128)(2,1)S(1)}, bf16[1,10,24,576]{3,2,0,1:T(8,128)(2,1)}, u32[]{:S(2)}) copy-start(bf16[1,10,24,576]{3,2,0,1:T(8,128)(2,1)} %stack.116) | copy-start | bytes 829444
  279.4 15.0 %copy-start.7 = (bf16[1,10,24,576]{3,2,0,1:T(8,128)(2,1)S(1)}, bf16[1,10,24,576]{3,2,0,1:T(8,128)(2,1)}, u32[]{:S(2)}) copy-start(bf16[1,10,24,576]{3,2,0,1:T(8,128)(2,1)} %stack.117) | copy-start | bytes 829444
  279.4 15.7 %copy-start.8 = (bf16[1,10,24,576]{3,2,0,1:T(8,128)(2,1)S(1)}, bf16[1,10,24,576]{3,2,0,1:T(8,128)(2,1)}, u32[]{:S(2)}) copy-start(bf16[1,10,24,576]{3,2,0,1:T(8,128)(2,1)} %stack.118) | copy-start | bytes 829444
  279.4 16.5 %copy-start.9 = (bf16[1,10,24,576]{3,2,0,1:T(8,128)(2,1)S(1)}, bf16[1,10,24,576]{3,2,0,1:T(8,128)(2,1)}, u32[]{:S(2)}) copy-start(bf16[1,10,24,576]{3,2,0,1:T(8,128)(2,1)} %stack.119) | copy-start | bytes 829444
  279.4 17.2 %copy-start.10 = (bf16[1,10,24,576]{3,2,0,1:T(8,128)(2,1)S(1)}, bf16[1,10,24,576]{3,2,0,1:T(8,128)(2,1)}, u32[]{:S(2)}) copy-start(bf16[1,10,24,576]{3,2,0,1:T(8,128)(2,1)} %stack.120) | copy-start | bytes 829444
  279.4 18.0 %copy-start.11 = (bf16[1,10,24,576]{3,2,0,1:T(8,128)(2,1)S(1)}, bf16[1,10,24,576]{3,2,0,1:T(8,128)(2,1)}, u32[]{:S(2)}) copy-start(bf16[1,10,24,576]{3,2,0,1:T(8,128)(2,1)} %stack.121) | copy-start | bytes 829444
  279.4 18.7 %copy-start.12 = (bf16[1,10,24,576]{3,2,0,1:T(8,128)(2,1)S(1)}, bf16[1,10,24,576]{3,2,0,1:T(8,128)(2,1)}, u32[]{:S(2)}) copy-start(bf16[1,10,24,576]{3,2,0,1:T(8,128)(2,1)} %stack.122) | copy-start | bytes 829444
  279.5 19.5 %copy-start.13 = (bf16[1,10,24,576]{3,2,0,1:T(8,128)(2,1)S(1)}, bf16[1,10,24,576]{3,2,0,1:T(8,128)(2,1)}, u32[]{:S(2)}) copy-start(bf16[1,10,24,576]{3,2,0,1:T(8,128)(2,1)} %stack.123) | copy-start | bytes 829444
  305.9 15.3 %copy-start = (f32[17,20,24,576]{3,2,1,0:T(8,128)}, f32[17,20,24,576]{3,2,1,0:T(8,128)S(1)}, u32[]{:S(2)}) copy-start(f32[17,20,24,576]{3,2,1,0:T(8,128)S(1)} %multiply_dynamic-update-slice_fusion) | copy-start | bytes 56401924
  305.9 15.3 %copy-start.17 = (f32[576,256,1,1]{1,0,3,2:T(8,128)S(1)}, f32[576,256,1,1]{1,0,3,2:T(8,128)}, u32[]{:S(2)}) copy-start(f32[576,256,1,1]{1,0,3,2:T(8,128)} %constant.259) | copy-start | bytes 1769476
  343.1 16.2 %copy-start.19 = (f32[256,16,1,1]{0,1,3,2:T(8,128)S(1)}, f32[256,16,1,1]{0,1,3,2:T(8,128)}, u32[]{:S(2)}) copy-start(f32[256,16,1,1]{0,1,3,2:T(8,128)} %constant.260) | copy-start | bytes 49156
  346.7 14.8 %copy-start.24 = (f32[16,24,1,1]{1,0,3,2:T(8,128)S(1)}, f32[16,24,1,1]{1,0,3,2:T(8,128)}, u32[]{:S(2)}) copy-start(f32[16,24,1,1]{1,0,3,2:T(8,128)} %constant.261) | copy-start | bytes 4612
  361.4 16.8 %copy-start.16 = (f32[576,256,1,1]{1,0,3,2:T(8,128)S(1)}, f32[576,256,1,1]{1,0,3,2:T(8,128)}, u32[]{:S(2)}) copy-start(f32[576,256,1,1]{1,0,3,2:T(8,128)} %constant.262) | copy-start | bytes 1769476
  401.6 14.8 %copy-start.23 = (f32[16,24,1,1]{1,0,3,2:T(8,128)S(1)}, f32[16,24,1,1]{1,0,3,2:T(8,128)}, u32[]{:S(2)}) copy-start(f32[16,24,1,1]{1,0,3,2:T(8,128)} %constant.263) | copy-start | bytes 4612
  416.4 16.7 %copy-start.15 = (f32[576,256,1,1]{1,0,3,2:T(8,128)S(1)}, f32[576,256,1,1]{1,0,3,2:T(8,128)}, u32[]{:S(2)}) copy-start(f32[576,256,1,1]{1,0,3,2:T(8,128)} %constant.264) | copy-start | bytes 1769476
  456.5 14.8 %copy-start.22 = (f32[16,24,1,1]{1,0,3,2:T(8,128)S(1)}, f32[16,24,1,1]{1,0,3,2:T(8,128)}, u32[]{:S(2)}) copy-start(f32[16,24,1,1]{1,0,3,2:T(8,128)} %constant.265) | copy-start | bytes 4612
  471.3 17.1 %copy-start.14 = (f32[576,256,1,1]{1,0,3,2:T(8,128)S(1)}, f32[576,256,1,1]{1,0,3,2:T(8,128)}, u32[]{:S(2)}) copy-start(f32[576,256,1,1]{1,0,3,2:T(8,128)} %constant.266) | copy-start | bytes 1769476
  515.4 11.5 %copy-start.26 = (pred[20]{0:T(512)(128)(4,1)S(1)}, pred[20]{0:T(512)(128)(4,1)}, u32[]{:S(2)}) copy-start(pred[20]{0:T(512)(128)(4,1)} %get-tuple-element.58) | copy-start | bytes 64
  524.4 53.3 %copy-start.18 = (f32[2560,32]{0,1:T(8,128)S(1)}, f32[2560,32]{0,1:T(8,128)}, u32[]{:S(2)}) copy-start(f32[2560,32]{0,1:T(8,128)} %fusion.28) | copy-start | bytes 983044
  524.4 53.3 %copy-start.21 = (f32[2560,4]{0,1:T(4,128)S(1)}, f32[2560,4]{0,1:T(4,128)}, u32[]{:S(2)}) copy-start(f32[2560,4]{0,1:T(4,128)} %convert_bitcast_fusion) | copy-start | bytes 122884
  524.4 53.3 %copy-start.28 = (f32[4,32]{1,0:T(4,128)S(1)}, f32[4,32]{1,0:T(4,128)}, u32[]{:S(2)}) copy-start(f32[4,32]{1,0:T(4,128)} %convolution_maximum_fusion) | copy-start | bytes 1540
  528.9 50.7 %all-to-all-start = ((f32[16,2,2048]{2,1,0:T(2,128)}), f32[16,2,2048]{2,1,0:T(2,128)S(1)}, u32[]{:S(2)}, u32[]{:S(2)}) async-start(f32[16,2,2048]{2,1,0:T(2,128)} %reshape.1067), calls=%async_computation | async-start | bytes 524288 | tf_op jit(solution)/shard_map/all_to_all | solution.py:173
  (2 other events, 5.7 us)

commit v6 on v5

--- a/solution.py
+++ b/solution.py
@@ -40,9 +40,20 @@
     return np.einsum("ax,by->xyab", weights, weights).reshape(span * span, TE * TE).astype(np.float32)
 
 
+def band_ones(half_width):
+    span = TE + 2 * HW
+    row_index = np.arange(TE)[:, None]
+    column_index = np.arange(span)[None, :]
+    return (np.abs(column_index - row_index - HW) <= half_width).astype(np.float32)
+
+
 def box_band(columns, half_width):
-    along_z = jnp.einsum("az,qtzp->qtap", band_matrix(half_width), columns, precision=HIGHEST)
-    return jnp.einsum("qtap,pc->qtac", along_z, plane_matrix(half_width), precision=HIGHEST)
+    window = 2 * half_width + 1
+    along_z = jnp.einsum(
+        "az,qtzp->qtap", band_ones(half_width), columns, precision=lax.Precision.HIGH
+    )
+    weights = (plane_matrix(half_width).astype(np.float64) / window).astype(np.float32)
+    return jnp.einsum("qtap,pc->qtac", along_z, weights, precision=HIGHEST)
 
 
 def quantities(tiles):

time: 589 us -> 599 us (1.017)
  other arithmetic: 66.9 us -> 78.6 us
  matrix products: 136 us -> 128 us
    unnamed x38, other arithmetic: 1.88 us -> 12.5 us
    dot_general x8, matrix products: 125 us -> 118 us  [the longest x4 65.3 us: box_band(): return jnp.einsum('qtap,pc->qtac', along_z, weights, precision=HIGHEST)]
    unnamed x86 -> x84, local copies, waits for them, and re-layouts: 41.8 us -> 47.8 us
where the time goes in v6:
time: 599 us; the launch traced here: 591 us
  local copies, waits for them, and re-layouts  288 us (48%)
  matrix products  128 us (21%)
  other arithmetic  78.6 us (13%)
  blocking collectives  40.3 us (7%)
  between operations  38 us (6%)
  starting transfers between devices  12 us (2%)
    dynamic_slice x24, local copies, waits for them, and re-layouts, cut_tiles(): lax.dynamic_slice(padded, (jnp.int32(0), depth_at[index] * TE, column_at[...  85.1 us
    dot_general x4, matrix products, box_band(): return jnp.einsum('qtap,pc->qtac', along_z, weights, precision=HIGHEST)  65.3 us
    another operation x21, local copies, waits for them, and re-layouts, cut_tiles(): return jnp.stack(pieces, axis=0)  53.8 us
    dot_general x4, matrix products, box_band(): jnp.einsum('az,qtzp->qtap', band_ones(half_width), columns, precision=lax...  52.5 us
    unnamed x84, local copies, waits for them, and re-layouts  47.8 us
    all_gather x1, blocking collectives, shards(): every_means = lax.all_gather(own_means, ('gx', 'gy'), axis=0, tiled=False)  40.3 us
    concatenate x1, other arithmetic, shards(): padded = jnp.concatenate([padded[:, -HW:], padded, padded[:, :HW]], axis=1)  34.7 us
    squeeze x12, local copies, waits for them, and re-layouts, closure_blocks(): smoothed[9 + direction]  21.5 us
  transfers between devices with their start and end apart: 5, of which 2 were waited for; matrix products, arithmetic and copies ran while one was open for 8% of the time, Pallas kernels for 0%

profile of v6, /device:TPU:1, one launch (start us, length us, event | category | flops | bytes accessed | tf_op | source)
XLA Modules:
  0.0 591.1 jit_solution(2897650829729779626)
XLA Ops:
  4.6 3.7 collective-permute-start.1
  14.4 15.6 %copy.287 = bf16[10,32,64,128]{2,1,3,0:T(8,128)(2,1)} copy(bf16[10,32,64,128]{3,2,1,0:T(8,128)(2,1)} %param.16) | data formatting | bytes 10485760 | tf_op args[0]
  67.5 3.4 scatter_custom_fusion.1
  73.5 7.9 %copy.286 = bf16[10,32,4,128]{2,1,3,0:T(8,128)(2,1)} copy(bf16[10,32,4,128]{3,1,2,0:T(8,128)(2,1)S(1)} %collective-permute-done) | data formatting | bytes 655360 | tf_op jit(solution)/shard_map/ppermute | solution.py:21
  81.4 7.8 %copy.288 = bf16[10,32,4,128]{2,1,3,0:T(8,128)(2,1)} copy(bf16[10,32,4,128]{3,1,2,0:T(8,128)(2,1)S(1)} %collective-permute-done.1) | data formatting | bytes 655360 | tf_op jit(solution)/shard_map/ppermute | solution.py:24
  94.5 3.4 collective-permute-done.2
  100.4 34.7 %fusion = bf16[10,40,72,136]{2,1,3,0:T(8,128)(2,1)S(1)} fusion(bf16[10,32,72,4]{2,1,3,0:T(8,128)(2,1)S(1)} %collective-permute-done.3, bf16[10,32,72,4]{2,1,3,0:T(8,128)(2,1)S(1)} %collective-permute-done.2, bf16[10,32,4,128]{2,1,3,0:T(8,128)(2,1)} %copy.288, bf16[10,32,64,128]{2,1,3,0:T(8,128)(2,1)} %copy.287, bf16[10,32,4,128]{2,1,3,0:T(8,128)(2,1)} %copy.286), kind=kLoop, calls=%fused_computation.4 | loop fusion | flops 117504000 | bytes 14100480 | tf_op jit(solution)/shard_map/concatenate | solution.py:148
  135.1 5.0 copy-done
  149.1 12.5 %constant_dynamic-slice_fusion.12 = (bf16[10,24,24,24]{2,1,3,0:T(8,128)(2,1)S(1)}, bf16[10,24,24,24]{2,1,3,0:T(8,128)(2,1)S(1)}, bf16[10,24,24,24]{2,1,3,0:T(8,1...) fusion(bf16[10,40,72,136]{2,1,3,0:T(8,128)(2,1)} %copy-done, ...), kind=kLoop, calls=%fused_computation.236 | loop fusion | bytes 3317832 | tf_op jit(solution)/shard_map/dynamic_slice | solution.py:129
  186.3 3.0 stack.110
  191.9 13.1 %constant_dynamic-slice_fusion.6 = (bf16[10,24,24,24]{2,1,3,0:T(8,128)(2,1)S(1)}, bf16[10,24,24,24]{2,1,3,0:T(8,128)(2,1)S(1)}, bf16[10,24,24,24]{2,1,3,0:T(8,12...) fusion(bf16[10,40,72,136]{2,1,3,0:T(8,128)(2,1)} %copy-done, ...), kind=kLoop, calls=%fused_computation.230 | loop fusion | bytes 3317832 | tf_op jit(solution)/shard_map/dynamic_slice | solution.py:129
  207.7 3.3 stack.112
  229.9 3.0 stack.116
  235.7 13.1 %constant_dynamic-slice_fusion = (bf16[10,24,24,24]{2,1,3,0:T(8,128)(2,1)S(1)}, bf16[10,24,24,24]{2,1,3,0:T(8,128)(2,1)S(1)}, bf16[10,24,24,24]{2,1,3,0:T(8,128)...) fusion(bf16[10,40,72,136]{2,1,3,0:T(8,128)(2,1)} %copy-done, ...), kind=kLoop, calls=%fused_computation.224 | loop fusion | bytes 3317832 | tf_op jit(solution)/shard_map/dynamic_slice | solution.py:129
  257.3 3.0 stack.119
  268.8 3.0 stack.121
  299.5 3.7 convert_element_type.23
  323.1 13.0 %fusion.62 = f32[17,20,576,16]{2,3,1,0:T(8,128)} fusion(f32[17,20,24,576]{3,2,1,0:T(8,128)} %multiply_dynamic-update-slice_fusion, f32[16,24,1,1]{1,0,3,2:T(8,128)S(1)} %copy-done.24), kind=kOutput, calls=%fused_computation.284 | convolution fusion | flops 451215360 | bytes 31335936 | tf_op jit(solution)/shard_map/az,qtzp->qtap/dot_general | solution.py:52
  336.1 16.5 %fusion.8 = f32[17,20,16,256]{3,2,1,0:T(8,128)S(1)} fusion(f32[576,256,1,1]{1,0,3,2:T(8,128)S(1)} %copy-done.16, f32[17,20,576,16]{2,3,1,0:T(8,128)} %fusion.62), kind=kOutput, calls=%fused_computation.19 | convolution fusion | flops 9625927680 | bytes 18694144 | tf_op jit(solution)/shard_map/qtap,pc->qtac/dot_general | solution.py:56
  369.6 4.3 subtract_reduce_fusion.21
  376.4 13.1 %fusion.64 = f32[17,20,576,16]{2,3,1,0:T(8,128)} fusion(f32[17,20,24,576]{3,2,1,0:T(8,128)} %multiply_dynamic-update-slice_fusion, f32[16,24,1,1]{1,0,3,2:T(8,128)S(1)} %copy-done.23), kind=kOutput, calls=%fused_computation.286 | convolution fusion | flops 451215360 | bytes 31335936 | tf_op jit(solution)/shard_map/az,qtzp->qtap/dot_general | solution.py:52
  389.5 16.3 %fusion.6 = f32[17,20,16,256]{3,2,1,0:T(8,128)S(1)} fusion(f32[576,256,1,1]{1,0,3,2:T(8,128)S(1)} %copy-done.15, f32[17,20,576,16]{2,3,1,0:T(8,128)} %fusion.64), kind=kOutput, calls=%fused_computation.17 | convolution fusion | flops 9625927680 | bytes 18694144 | tf_op jit(solution)/shard_map/qtap,pc->qtac/dot_general | solution.py:56
  422.8 4.3 subtract_reduce_fusion.14
  429.6 13.0 %fusion.66 = f32[17,20,576,16]{2,3,1,0:T(8,128)} fusion(f32[17,20,24,576]{3,2,1,0:T(8,128)} %multiply_dynamic-update-slice_fusion, f32[16,24,1,1]{1,0,3,2:T(8,128)S(1)} %copy-done.22), kind=kOutput, calls=%fused_computation.288 | convolution fusion | flops 451215360 | bytes 31335936 | tf_op jit(solution)/shard_map/az,qtzp->qtap/dot_general | solution.py:52
  442.6 16.3 %fusion.4 = f32[17,20,16,256]{3,2,1,0:T(8,128)S(1)} fusion(f32[576,256,1,1]{1,0,3,2:T(8,128)S(1)} %copy-done.14, f32[17,20,576,16]{2,3,1,0:T(8,128)} %fusion.66), kind=kOutput, calls=%fused_computation.15 | convolution fusion | flops 9625927680 | bytes 18694144 | tf_op jit(solution)/shard_map/qtap,pc->qtac/dot_general | solution.py:56
  475.9 4.3 subtract_reduce_fusion.7
  482.7 13.4 %fusion.68 = f32[17,20,576,16]{2,3,1,0:T(8,128)} fusion(f32[17,20,24,576]{3,2,1,0:T(8,128)} %multiply_dynamic-update-slice_fusion, f32[16,24,1,1]{1,0,3,2:T(8,128)S(1)} %copy-done.21), kind=kOutput, calls=%fused_computation.290 | convolution fusion | flops 451215360 | bytes 31335936 | tf_op jit(solution)/shard_map/az,qtzp->qtap/dot_general | solution.py:52
  496.1 16.2 %fusion.2 = f32[17,20,16,256]{3,2,1,0:T(8,128)S(1)} fusion(f32[576,256,1,1]{1,0,3,2:T(8,128)S(1)} %copy-done.13, f32[17,20,576,16]{2,3,1,0:T(8,128)} %fusion.68), kind=kOutput, calls=%fused_computation.13 | convolution fusion | flops 9625927680 | bytes 18694144 | tf_op jit(solution)/shard_map/qtap,pc->qtac/dot_general | solution.py:56
  529.4 4.3 subtract_reduce_fusion
  538.5 3.5 all-to-all-start
  542.1 40.3 %all_gather.4 = f32[128,20,32]{2,1,0:T(8,128)} all-gather(f32[1,20,32]{2,1,0:T(8,128)S(1)} %copy.347), channel_id=1, replica_groups=mesh['gx'=16,'gy'=8] {'gx','gy'}, dimensions={0}, use_global_device_ids=true | all-gather | bytes 330240 | tf_op jit(solution)/shard_map/all_gather | solution.py:191
  582.4 3.4 copy.349
  (301 shorter events, 231.5 us)
Async XLA Ops:
  2.3 71.2 %collective-permute-start = (bf16[10,32,4,128]{3,1,2,0:T(8,128)(2,1)S(1)}, bf16[10,32,4,128]{3,1,2,0:T(8,128)(2,1)S(1)}, u32[]{:S(2)}, u32[]{:S(2)}) collective-permute-start(bf16[10,32,4,128]{3,1,2,0:T(8,128)(2,1)S(1)} %copy.360), channel_id=1, source_target_pairs={{0,8},{8,16},{16,24},{24,32},{32,40},{40,48},{48,56},{56,64},{64,7... | collective-permute-start | bytes 983048 | tf_op jit(solution)/shard_map/ppermute | solution.py:21
  4.6 76.9 %collective-permute-start.1 = (bf16[10,32,4,128]{3,1,2,0:T(8,128)(2,1)S(1)}, bf16[10,32,4,128]{3,1,2,0:T(8,128)(2,1)S(1)}, u32[]{:S(2)}, u32[]{:S(2)}) collective-permute-start(bf16[10,32,4,128]{3,1,2,0:T(8,128)(2,1)S(1)} %copy.361), channel_id=1, source_target_pairs={{8,0},{16,8},{24,16},{32,24},{40,32},{48,40},{56,48},{64,56},{72,6... | collective-permute-start | bytes 983048 | tf_op jit(solution)/shard_map/ppermute | solution.py:24
  14.4 49.3 %copy-start.19 = (s32[8,16,20]{2,1,0:T(8,128)S(1)}, s32[8,16,20]{2,1,0:T(8,128)}, u32[]{:S(2)}) copy-start(s32[8,16,20]{2,1,0:T(8,128)} %param.17) | copy-start | bytes 30724
  14.4 56.9 %copy-start.26 = (s32[32]{0:T(128)S(1)}, s32[32]{0:T(128)}, u32[]{:S(2)}) copy-start(s32[32]{0:T(128)} %param.19) | copy-start | bytes 388
  91.3 6.6 %collective-permute-start.2 = (bf16[10,32,72,4]{2,1,3,0:T(8,128)(2,1)S(1)}, bf16[10,32,72,4]{2,1,3,0:T(8,128)(2,1)S(1)}, u32[]{:S(2)}, u32[]{:S(2)}) collective-permute-start(bf16[10,32,72,4]{2,1,3,0:T(8,128)(2,1)S(1)} %get-tuple-element.62), channel_id=1, source_target_pairs={{0,1},{1,2},{2,3},{3,4},{4,5},{5,6},{6,7},{7,0},{8,9},{9,10},{10,1... | collective-permute-start | bytes 552968 | tf_op jit(solution)/shard_map/ppermute | solution.py:21
  93.9 6.5 %collective-permute-start.3 = (bf16[10,32,72,4]{2,1,3,0:T(8,128)(2,1)S(1)}, bf16[10,32,72,4]{2,1,3,0:T(8,128)(2,1)S(1)}, u32[]{:S(2)}, u32[]{:S(2)}) collective-permute-start(bf16[10,32,72,4]{2,1,3,0:T(8,128)(2,1)S(1)} %get-tuple-element.63), channel_id=1, source_target_pairs={{1,0},{2,1},{3,2},{4,3},{5,4},{6,5},{7,6},{0,7},{9,8},{10,9},{11,1... | collective-permute-start | bytes 552968 | tf_op jit(solution)/shard_map/ppermute | solution.py:24
  135.1 5.0 copy-start
  277.5 12.9 %copy-start.1 = (bf16[1,10,24,576]{3,2,0,1:T(8,128)(2,1)S(1)}, bf16[1,10,24,576]{3,2,0,1:T(8,128)(2,1)}, u32[]{:S(2)}) copy-start(bf16[1,10,24,576]{3,2,0,1:T(8,128)(2,1)} %stack.112) | copy-start | bytes 829444
  277.5 13.6 %copy-start.2 = (bf16[1,10,24,576]{3,2,0,1:T(8,128)(2,1)S(1)}, bf16[1,10,24,576]{3,2,0,1:T(8,128)(2,1)}, u32[]{:S(2)}) copy-start(bf16[1,10,24,576]{3,2,0,1:T(8,128)(2,1)} %stack.113) | copy-start | bytes 829444
  277.5 14.4 %copy-start.3 = (bf16[1,10,24,576]{3,2,0,1:T(8,128)(2,1)S(1)}, bf16[1,10,24,576]{3,2,0,1:T(8,128)(2,1)}, u32[]{:S(2)}) copy-start(bf16[1,10,24,576]{3,2,0,1:T(8,128)(2,1)} %stack.114) | copy-start | bytes 829444
  277.5 15.1 %copy-start.4 = (bf16[1,10,24,576]{3,2,0,1:T(8,128)(2,1)S(1)}, bf16[1,10,24,576]{3,2,0,1:T(8,128)(2,1)}, u32[]{:S(2)}) copy-start(bf16[1,10,24,576]{3,2,0,1:T(8,128)(2,1)} %stack.115) | copy-start | bytes 829444
  279.2 14.2 %copy-start.5 = (bf16[1,10,24,576]{3,2,0,1:T(8,128)(2,1)S(1)}, bf16[1,10,24,576]{3,2,0,1:T(8,128)(2,1)}, u32[]{:S(2)}) copy-start(bf16[1,10,24,576]{3,2,0,1:T(8,128)(2,1)} %stack.116) | copy-start | bytes 829444
  279.2 15.0 %copy-start.6 = (bf16[1,10,24,576]{3,2,0,1:T(8,128)(2,1)S(1)}, bf16[1,10,24,576]{3,2,0,1:T(8,128)(2,1)}, u32[]{:S(2)}) copy-start(bf16[1,10,24,576]{3,2,0,1:T(8,128)(2,1)} %stack.117) | copy-start | bytes 829444
  279.2 15.7 %copy-start.7 = (bf16[1,10,24,576]{3,2,0,1:T(8,128)(2,1)S(1)}, bf16[1,10,24,576]{3,2,0,1:T(8,128)(2,1)}, u32[]{:S(2)}) copy-start(bf16[1,10,24,576]{3,2,0,1:T(8,128)(2,1)} %stack.118) | copy-start | bytes 829444
  279.2 16.5 %copy-start.8 = (bf16[1,10,24,576]{3,2,0,1:T(8,128)(2,1)S(1)}, bf16[1,10,24,576]{3,2,0,1:T(8,128)(2,1)}, u32[]{:S(2)}) copy-start(bf16[1,10,24,576]{3,2,0,1:T(8,128)(2,1)} %stack.119) | copy-start | bytes 829444
  279.2 17.2 %copy-start.9 = (bf16[1,10,24,576]{3,2,0,1:T(8,128)(2,1)S(1)}, bf16[1,10,24,576]{3,2,0,1:T(8,128)(2,1)}, u32[]{:S(2)}) copy-start(bf16[1,10,24,576]{3,2,0,1:T(8,128)(2,1)} %stack.120) | copy-start | bytes 829444
  279.2 18.0 %copy-start.10 = (bf16[1,10,24,576]{3,2,0,1:T(8,128)(2,1)S(1)}, bf16[1,10,24,576]{3,2,0,1:T(8,128)(2,1)}, u32[]{:S(2)}) copy-start(bf16[1,10,24,576]{3,2,0,1:T(8,128)(2,1)} %stack.121) | copy-start | bytes 829444
  279.2 18.7 %copy-start.11 = (bf16[1,10,24,576]{3,2,0,1:T(8,128)(2,1)S(1)}, bf16[1,10,24,576]{3,2,0,1:T(8,128)(2,1)}, u32[]{:S(2)}) copy-start(bf16[1,10,24,576]{3,2,0,1:T(8,128)(2,1)} %stack.122) | copy-start | bytes 829444
  279.3 19.5 %copy-start.12 = (bf16[1,10,24,576]{3,2,0,1:T(8,128)(2,1)S(1)}, bf16[1,10,24,576]{3,2,0,1:T(8,128)(2,1)}, u32[]{:S(2)}) copy-start(bf16[1,10,24,576]{3,2,0,1:T(8,128)(2,1)} %stack.123) | copy-start | bytes 829444
  323.1 13.0 %copy-start.16 = (f32[576,256,1,1]{1,0,3,2:T(8,128)S(1)}, f32[576,256,1,1]{1,0,3,2:T(8,128)}, u32[]{:S(2)}) copy-start(f32[576,256,1,1]{1,0,3,2:T(8,128)} %constant.259) | copy-start | bytes 1769476
  358.0 16.2 %copy-start.18 = (f32[256,16,1,1]{0,1,3,2:T(8,128)S(1)}, f32[256,16,1,1]{0,1,3,2:T(8,128)}, u32[]{:S(2)}) copy-start(f32[256,16,1,1]{0,1,3,2:T(8,128)} %constant.260) | copy-start | bytes 49156
  361.6 14.8 %copy-start.23 = (f32[16,24,1,1]{1,0,3,2:T(8,128)S(1)}, f32[16,24,1,1]{1,0,3,2:T(8,128)}, u32[]{:S(2)}) copy-start(f32[16,24,1,1]{1,0,3,2:T(8,128)} %constant.261) | copy-start | bytes 4612
  376.4 13.1 %copy-start.15 = (f32[576,256,1,1]{1,0,3,2:T(8,128)S(1)}, f32[576,256,1,1]{1,0,3,2:T(8,128)}, u32[]{:S(2)}) copy-start(f32[576,256,1,1]{1,0,3,2:T(8,128)} %constant.262) | copy-start | bytes 1769476
  414.8 14.8 %copy-start.22 = (f32[16,24,1,1]{1,0,3,2:T(8,128)S(1)}, f32[16,24,1,1]{1,0,3,2:T(8,128)}, u32[]{:S(2)}) copy-start(f32[16,24,1,1]{1,0,3,2:T(8,128)} %constant.263) | copy-start | bytes 4612
  429.6 13.0 %copy-start.14 = (f32[576,256,1,1]{1,0,3,2:T(8,128)S(1)}, f32[576,256,1,1]{1,0,3,2:T(8,128)}, u32[]{:S(2)}) copy-start(f32[576,256,1,1]{1,0,3,2:T(8,128)} %constant.264) | copy-start | bytes 1769476
  467.9 14.8 %copy-start.21 = (f32[16,24,1,1]{1,0,3,2:T(8,128)S(1)}, f32[16,24,1,1]{1,0,3,2:T(8,128)}, u32[]{:S(2)}) copy-start(f32[16,24,1,1]{1,0,3,2:T(8,128)} %constant.265) | copy-start | bytes 4612
  482.7 13.4 %copy-start.13 = (f32[576,256,1,1]{1,0,3,2:T(8,128)S(1)}, f32[576,256,1,1]{1,0,3,2:T(8,128)}, u32[]{:S(2)}) copy-start(f32[576,256,1,1]{1,0,3,2:T(8,128)} %constant.266) | copy-start | bytes 1769476
  525.0 11.5 %copy-start.25 = (pred[20]{0:T(512)(128)(4,1)S(1)}, pred[20]{0:T(512)(128)(4,1)}, u32[]{:S(2)}) copy-start(pred[20]{0:T(512)(128)(4,1)} %get-tuple-element.58) | copy-start | bytes 64
  534.0 53.5 %copy-start.17 = (f32[2560,32]{0,1:T(8,128)S(1)}, f32[2560,32]{0,1:T(8,128)}, u32[]{:S(2)}) copy-start(f32[2560,32]{0,1:T(8,128)} %fusion.28) | copy-start | bytes 983044
  534.0 53.5 %copy-start.20 = (f32[2560,4]{0,1:T(4,128)S(1)}, f32[2560,4]{0,1:T(4,128)}, u32[]{:S(2)}) copy-start(f32[2560,4]{0,1:T(4,128)} %convert_bitcast_fusion) | copy-start | bytes 122884
  534.0 53.5 %copy-start.27 = (f32[4,32]{1,0:T(4,128)S(1)}, f32[4,32]{1,0:T(4,128)}, u32[]{:S(2)}) copy-start(f32[4,32]{1,0:T(4,128)} %convolution_maximum_fusion) | copy-start | bytes 1540
  538.5 50.9 %all-to-all-start = ((f32[16,2,2048]{2,1,0:T(2,128)}), f32[16,2,2048]{2,1,0:T(2,128)S(1)}, u32[]{:S(2)}, u32[]{:S(2)}) async-start(f32[16,2,2048]{2,1,0:T(2,128)} %reshape.1067), calls=%async_computation | async-start | bytes 524288 | tf_op jit(solution)/shard_map/all_to_all | solution.py:184
  (1 other events, 2.4 us)

commit v7 on v5

--- a/solution.py
+++ b/solution.py
@@ -177,7 +177,9 @@
         jnp.mean(own_statistics.reshape(list_length, HW * 8, stat_length // (HW * 8)), axis=2),
         0.0,
     )
-    every_means = lax.all_gather(own_means, ("gx", "gy"), axis=0, tiled=False)
+    every_means = lax.all_gather(
+        lax.all_gather(own_means, "gy", axis=0, tiled=False), "gx", axis=0, tiled=False
+    )
     every_means = jnp.transpose(
         every_means.reshape(groups_x, groups_y, list_length, HW * 8), (1, 0, 2, 3)
     ).reshape(groups_y * groups_x * list_length, HW * 8)

time: 589 us -> 590 us (level)
    all_gather x1 -> x2, blocking collectives: 40.1 us -> 37.9 us  [the longest x1 25.5 us: shards(): lax.all_gather(lax.all_gather(own_means, 'gy', axis=0, tiled=False), 'gx'...]
    unnamed x86 -> x82, local copies, waits for them, and re-layouts: 41.8 us -> 41.8 us
where the time goes in v7:
time: 590 us; the launch traced here: 581 us
  local copies, waits for them, and re-layouts  282 us (48%)
  matrix products  137 us (23%)
  other arithmetic  66.9 us (11%)
  between operations  38.1 us (6%)
  blocking collectives  37.9 us (6%)
  starting transfers between devices  12.7 us (2%)
  waiting for transfers between devices  5.92 us (1%)
    dynamic_slice x24, local copies, waits for them, and re-layouts, cut_tiles(): lax.dynamic_slice(padded, (jnp.int32(0), depth_at[index] * TE, column_at[...  85.3 us
    dot_general x4, matrix products, box_band(): jnp.einsum('az,qtzp->qtap', band_matrix(half_width), columns, precision=H...  65.8 us
    dot_general x4, matrix products, box_band(): jnp.einsum('qtap,pc->qtac', along_z, plane_matrix(half_width), precision=...  59.6 us
    another operation x21, local copies, waits for them, and re-layouts, cut_tiles(): return jnp.stack(pieces, axis=0)  53.8 us
    unnamed x82, local copies, waits for them, and re-layouts  41.8 us
    concatenate x1, other arithmetic, shards(): padded = jnp.concatenate([padded[:, -HW:], padded, padded[:, :HW]], axis=1)  34.7 us
    all_gather x1, blocking collectives, shards(): lax.all_gather(lax.all_gather(own_means, 'gy', axis=0, tiled=False), 'gx'...  25.5 us
    squeeze x12, local copies, waits for them, and re-layouts, closure_blocks(): smoothed[9 + direction]  21.5 us
  transfers between devices with their start and end apart: 5, of which 2 were waited for; matrix products, arithmetic and copies ran while one was open for 8% of the time, Pallas kernels for 0%

profile of v7, /device:TPU:1, one launch (start us, length us, event | category | flops | bytes accessed | tf_op | source)
XLA Modules:
  0.0 580.6 jit_solution(13322583176380739177)
XLA Ops:
  4.6 3.7 collective-permute-start.1
  14.4 15.6 %copy.287 = bf16[10,32,64,128]{2,1,3,0:T(8,128)(2,1)} copy(bf16[10,32,64,128]{3,2,1,0:T(8,128)(2,1)} %param.16) | data formatting | bytes 10485760 | tf_op args[0]
  67.5 3.4 scatter_custom_fusion.1
  73.5 7.9 %copy.286 = bf16[10,32,4,128]{2,1,3,0:T(8,128)(2,1)} copy(bf16[10,32,4,128]{3,1,2,0:T(8,128)(2,1)S(1)} %collective-permute-done) | data formatting | bytes 655360 | tf_op jit(solution)/shard_map/ppermute | solution.py:21
  81.4 7.8 %copy.288 = bf16[10,32,4,128]{2,1,3,0:T(8,128)(2,1)} copy(bf16[10,32,4,128]{3,1,2,0:T(8,128)(2,1)S(1)} %collective-permute-done.1) | data formatting | bytes 655360 | tf_op jit(solution)/shard_map/ppermute | solution.py:24
  94.5 3.4 collective-permute-done.2
  100.4 34.7 %fusion = bf16[10,40,72,136]{2,1,3,0:T(8,128)(2,1)S(1)} fusion(bf16[10,32,72,4]{2,1,3,0:T(8,128)(2,1)S(1)} %collective-permute-done.3, bf16[10,32,72,4]{2,1,3,0:T(8,128)(2,1)S(1)} %collective-permute-done.2, bf16[10,32,4,128]{2,1,3,0:T(8,128)(2,1)} %copy.288, bf16[10,32,64,128]{2,1,3,0:T(8,128)(2,1)} %copy.287, bf16[10,32,4,128]{2,1,3,0:T(8,128)(2,1)} %copy.286), kind=kLoop, calls=%fused_computation.4 | loop fusion | flops 117504000 | bytes 14100480 | tf_op jit(solution)/shard_map/concatenate | solution.py:137
  135.1 5.0 copy-done.1
  149.1 12.7 %constant_dynamic-slice_fusion.12 = (bf16[10,24,24,24]{2,1,3,0:T(8,128)(2,1)S(1)}, bf16[10,24,24,24]{2,1,3,0:T(8,128)(2,1)S(1)}, bf16[10,24,24,24]{2,1,3,0:T(8,1...) fusion(bf16[10,40,72,136]{2,1,3,0:T(8,128)(2,1)} %copy-done.1, ...), kind=kLoop, calls=%fused_computation.236 | loop fusion | bytes 3317832 | tf_op jit(solution)/shard_map/dynamic_slice | solution.py:118
  186.5 3.0 stack.110
  192.1 13.1 %constant_dynamic-slice_fusion.6 = (bf16[10,24,24,24]{2,1,3,0:T(8,128)(2,1)S(1)}, bf16[10,24,24,24]{2,1,3,0:T(8,128)(2,1)S(1)}, bf16[10,24,24,24]{2,1,3,0:T(8,12...) fusion(bf16[10,40,72,136]{2,1,3,0:T(8,128)(2,1)} %copy-done.1, ...), kind=kLoop, calls=%fused_computation.230 | loop fusion | bytes 3317832 | tf_op jit(solution)/shard_map/dynamic_slice | solution.py:118
  207.9 3.3 stack.112
  230.1 3.0 stack.116
  235.9 13.1 %constant_dynamic-slice_fusion = (bf16[10,24,24,24]{2,1,3,0:T(8,128)(2,1)S(1)}, bf16[10,24,24,24]{2,1,3,0:T(8,128)(2,1)S(1)}, bf16[10,24,24,24]{2,1,3,0:T(8,128)...) fusion(bf16[10,40,72,136]{2,1,3,0:T(8,128)(2,1)} %copy-done.1, ...), kind=kLoop, calls=%fused_computation.224 | loop fusion | bytes 3317832 | tf_op jit(solution)/shard_map/dynamic_slice | solution.py:118
  257.5 3.0 stack.119
  269.0 3.0 stack.121
  299.7 3.7 convert_element_type.23
  305.9 15.3 %fusion.62 = f32[17,20,576,16]{2,3,1,0:T(8,128)} fusion(f32[17,20,24,576]{3,2,1,0:T(8,128)S(1)} %multiply_dynamic-update-slice_fusion, f32[16,24,1,1]{1,0,3,2:T(8,128)S(1)} %copy-done.23), kind=kOutput, calls=%fused_computation.284 | convolution fusion | flops 902430720 | bytes 31335936 | tf_op jit(solution)/shard_map/az,qtzp->qtap/dot_general | solution.py:44
  321.2 16.4 %fusion.8 = f32[17,20,16,256]{3,2,1,0:T(8,128)S(1)} fusion(f32[576,256,1,1]{1,0,3,2:T(8,128)S(1)} %copy-done.17, f32[17,20,576,16]{2,3,1,0:T(8,128)} %fusion.62), kind=kOutput, calls=%fused_computation.19 | convolution fusion | flops 9625927680 | bytes 18694144 | tf_op jit(solution)/shard_map/qtap,pc->qtac/dot_general | solution.py:45
  354.7 4.3 subtract_reduce_fusion.21
  361.4 16.8 %fusion.64 = f32[17,20,576,16]{2,3,1,0:T(8,128)S(1)} fusion(f32[17,20,24,576]{3,2,1,0:T(8,128)} %copy-done, f32[16,24,1,1]{1,0,3,2:T(8,128)S(1)} %copy-done.22), kind=kOutput, calls=%fused_computation.286 | convolution fusion | flops 902430720 | bytes 31335936 | tf_op jit(solution)/shard_map/az,qtzp->qtap/dot_general | solution.py:44
  378.3 14.4 %fusion.6 = f32[17,20,16,256]{3,2,1,0:T(8,128)S(1)} fusion(f32[576,256,1,1]{1,0,3,2:T(8,128)S(1)} %copy-done.16, f32[17,20,576,16]{2,3,1,0:T(8,128)S(1)} %fusion.64), kind=kOutput, calls=%fused_computation.17 | convolution fusion | flops 9625927680 | bytes 18694144 | tf_op jit(solution)/shard_map/qtap,pc->qtac/dot_general | solution.py:45
  409.7 4.3 subtract_reduce_fusion.14
  416.4 16.7 %fusion.66 = f32[17,20,576,16]{2,3,1,0:T(8,128)S(1)} fusion(f32[17,20,24,576]{3,2,1,0:T(8,128)} %copy-done, f32[16,24,1,1]{1,0,3,2:T(8,128)S(1)} %copy-done.21), kind=kOutput, calls=%fused_computation.288 | convolution fusion | flops 902430720 | bytes 31335936 | tf_op jit(solution)/shard_map/az,qtzp->qtap/dot_general | solution.py:44
  433.1 14.4 %fusion.4 = f32[17,20,16,256]{3,2,1,0:T(8,128)S(1)} fusion(f32[576,256,1,1]{1,0,3,2:T(8,128)S(1)} %copy-done.15, f32[17,20,576,16]{2,3,1,0:T(8,128)S(1)} %fusion.66), kind=kOutput, calls=%fused_computation.15 | convolution fusion | flops 9625927680 | bytes 18694144 | tf_op jit(solution)/shard_map/qtap,pc->qtac/dot_general | solution.py:45
  464.6 4.3 subtract_reduce_fusion.7
  471.3 17.1 %fusion.68 = f32[17,20,576,16]{2,3,1,0:T(8,128)S(1)} fusion(f32[17,20,24,576]{3,2,1,0:T(8,128)} %copy-done, f32[16,24,1,1]{1,0,3,2:T(8,128)S(1)} %copy-done.20), kind=kOutput, calls=%fused_computation.290 | convolution fusion | flops 902430720 | bytes 31335936 | tf_op jit(solution)/shard_map/az,qtzp->qtap/dot_general | solution.py:44
  488.4 14.3 %fusion.2 = f32[17,20,16,256]{3,2,1,0:T(8,128)S(1)} fusion(f32[576,256,1,1]{1,0,3,2:T(8,128)S(1)} %copy-done.14, f32[17,20,576,16]{2,3,1,0:T(8,128)S(1)} %fusion.68), kind=kOutput, calls=%fused_computation.13 | convolution fusion | flops 9625927680 | bytes 18694144 | tf_op jit(solution)/shard_map/qtap,pc->qtac/dot_general | solution.py:45
  519.8 4.3 subtract_reduce_fusion
  527.0 12.4 %all_gather.10 = f32[8,20,32]{2,1,0:T(8,128)S(1)} all-gather(f32[1,20,32]{2,1,0:T(8,128)S(1)} %copy.347), channel_id=1, replica_groups=mesh['gx'=16,'gy'=8] {'gy'}, dimensions={0}, use_global_device_ids=true | all-gather | bytes 23040 | tf_op jit(solution)/shard_map/all_gather | solution.py:181
  541.4 4.2 all-to-all-start
  545.6 25.5 %all-gather = f32[128,20,32]{2,0,1:T(8,128)S(1)} all-gather(f32[8,20,32]{2,0,1:T(8,128)S(1)} %copy.348), channel_id=2, replica_groups=mesh['gx'=16,'gy'=8] {'gx'}, dimensions={0}, use_global_device_ids=true | all-gather | bytes 348160 | tf_op jit(solution)/shard_map/all_gather | solution.py:180
  (301 shorter events, 218.2 us)
Async XLA Ops:
  2.3 71.2 %collective-permute-start = (bf16[10,32,4,128]{3,1,2,0:T(8,128)(2,1)S(1)}, bf16[10,32,4,128]{3,1,2,0:T(8,128)(2,1)S(1)}, u32[]{:S(2)}, u32[]{:S(2)}) collective-permute-start(bf16[10,32,4,128]{3,1,2,0:T(8,128)(2,1)S(1)} %copy.359), channel_id=1, source_target_pairs={{0,8},{8,16},{16,24},{24,32},{32,40},{40,48},{48,56},{56,64},{64,7... | collective-permute-start | bytes 983048 | tf_op jit(solution)/shard_map/ppermute | solution.py:21
  4.6 76.9 %collective-permute-start.1 = (bf16[10,32,4,128]{3,1,2,0:T(8,128)(2,1)S(1)}, bf16[10,32,4,128]{3,1,2,0:T(8,128)(2,1)S(1)}, u32[]{:S(2)}, u32[]{:S(2)}) collective-permute-start(bf16[10,32,4,128]{3,1,2,0:T(8,128)(2,1)S(1)} %copy.360), channel_id=1, source_target_pairs={{8,0},{16,8},{24,16},{32,24},{40,32},{48,40},{56,48},{64,56},{72,6... | collective-permute-start | bytes 983048 | tf_op jit(solution)/shard_map/ppermute | solution.py:24
  14.4 49.3 %copy-start.19 = (s32[8,16,20]{2,1,0:T(8,128)S(1)}, s32[8,16,20]{2,1,0:T(8,128)}, u32[]{:S(2)}) copy-start(s32[8,16,20]{2,1,0:T(8,128)} %param.17) | copy-start | bytes 30724
  14.4 56.9 %copy-start.25 = (s32[32]{0:T(128)S(1)}, s32[32]{0:T(128)}, u32[]{:S(2)}) copy-start(s32[32]{0:T(128)} %param.19) | copy-start | bytes 388
  91.3 6.6 %collective-permute-start.2 = (bf16[10,32,72,4]{2,1,3,0:T(8,128)(2,1)S(1)}, bf16[10,32,72,4]{2,1,3,0:T(8,128)(2,1)S(1)}, u32[]{:S(2)}, u32[]{:S(2)}) collective-permute-start(bf16[10,32,72,4]{2,1,3,0:T(8,128)(2,1)S(1)} %get-tuple-element.62), channel_id=1, source_target_pairs={{0,1},{1,2},{2,3},{3,4},{4,5},{5,6},{6,7},{7,0},{8,9},{9,10},{10,1... | collective-permute-start | bytes 552968 | tf_op jit(solution)/shard_map/ppermute | solution.py:21
  93.9 6.5 %collective-permute-start.3 = (bf16[10,32,72,4]{2,1,3,0:T(8,128)(2,1)S(1)}, bf16[10,32,72,4]{2,1,3,0:T(8,128)(2,1)S(1)}, u32[]{:S(2)}, u32[]{:S(2)}) collective-permute-start(bf16[10,32,72,4]{2,1,3,0:T(8,128)(2,1)S(1)} %get-tuple-element.63), channel_id=1, source_target_pairs={{1,0},{2,1},{3,2},{4,3},{5,4},{6,5},{7,6},{0,7},{9,8},{10,9},{11,1... | collective-permute-start | bytes 552968 | tf_op jit(solution)/shard_map/ppermute | solution.py:24
  135.1 5.0 copy-start.1
  277.7 12.9 %copy-start.2 = (bf16[1,10,24,576]{3,2,0,1:T(8,128)(2,1)S(1)}, bf16[1,10,24,576]{3,2,0,1:T(8,128)(2,1)}, u32[]{:S(2)}) copy-start(bf16[1,10,24,576]{3,2,0,1:T(8,128)(2,1)} %stack.112) | copy-start | bytes 829444
  277.7 13.6 %copy-start.3 = (bf16[1,10,24,576]{3,2,0,1:T(8,128)(2,1)S(1)}, bf16[1,10,24,576]{3,2,0,1:T(8,128)(2,1)}, u32[]{:S(2)}) copy-start(bf16[1,10,24,576]{3,2,0,1:T(8,128)(2,1)} %stack.113) | copy-start | bytes 829444
  277.7 14.4 %copy-start.4 = (bf16[1,10,24,576]{3,2,0,1:T(8,128)(2,1)S(1)}, bf16[1,10,24,576]{3,2,0,1:T(8,128)(2,1)}, u32[]{:S(2)}) copy-start(bf16[1,10,24,576]{3,2,0,1:T(8,128)(2,1)} %stack.114) | copy-start | bytes 829444
  277.7 15.1 %copy-start.5 = (bf16[1,10,24,576]{3,2,0,1:T(8,128)(2,1)S(1)}, bf16[1,10,24,576]{3,2,0,1:T(8,128)(2,1)}, u32[]{:S(2)}) copy-start(bf16[1,10,24,576]{3,2,0,1:T(8,128)(2,1)} %stack.115) | copy-start | bytes 829444
  279.4 14.2 %copy-start.6 = (bf16[1,10,24,576]{3,2,0,1:T(8,128)(2,1)S(1)}, bf16[1,10,24,576]{3,2,0,1:T(8,128)(2,1)}, u32[]{:S(2)}) copy-start(bf16[1,10,24,576]{3,2,0,1:T(8,128)(2,1)} %stack.116) | copy-start | bytes 829444
  279.4 15.0 %copy-start.7 = (bf16[1,10,24,576]{3,2,0,1:T(8,128)(2,1)S(1)}, bf16[1,10,24,576]{3,2,0,1:T(8,128)(2,1)}, u32[]{:S(2)}) copy-start(bf16[1,10,24,576]{3,2,0,1:T(8,128)(2,1)} %stack.117) | copy-start | bytes 829444
  279.4 15.7 %copy-start.8 = (bf16[1,10,24,576]{3,2,0,1:T(8,128)(2,1)S(1)}, bf16[1,10,24,576]{3,2,0,1:T(8,128)(2,1)}, u32[]{:S(2)}) copy-start(bf16[1,10,24,576]{3,2,0,1:T(8,128)(2,1)} %stack.118) | copy-start | bytes 829444
  279.4 16.5 %copy-start.9 = (bf16[1,10,24,576]{3,2,0,1:T(8,128)(2,1)S(1)}, bf16[1,10,24,576]{3,2,0,1:T(8,128)(2,1)}, u32[]{:S(2)}) copy-start(bf16[1,10,24,576]{3,2,0,1:T(8,128)(2,1)} %stack.119) | copy-start | bytes 829444
  279.4 17.2 %copy-start.10 = (bf16[1,10,24,576]{3,2,0,1:T(8,128)(2,1)S(1)}, bf16[1,10,24,576]{3,2,0,1:T(8,128)(2,1)}, u32[]{:S(2)}) copy-start(bf16[1,10,24,576]{3,2,0,1:T(8,128)(2,1)} %stack.120) | copy-start | bytes 829444
  279.4 18.0 %copy-start.11 = (bf16[1,10,24,576]{3,2,0,1:T(8,128)(2,1)S(1)}, bf16[1,10,24,576]{3,2,0,1:T(8,128)(2,1)}, u32[]{:S(2)}) copy-start(bf16[1,10,24,576]{3,2,0,1:T(8,128)(2,1)} %stack.121) | copy-start | bytes 829444
  279.4 18.7 %copy-start.12 = (bf16[1,10,24,576]{3,2,0,1:T(8,128)(2,1)S(1)}, bf16[1,10,24,576]{3,2,0,1:T(8,128)(2,1)}, u32[]{:S(2)}) copy-start(bf16[1,10,24,576]{3,2,0,1:T(8,128)(2,1)} %stack.122) | copy-start | bytes 829444
  279.5 19.5 %copy-start.13 = (bf16[1,10,24,576]{3,2,0,1:T(8,128)(2,1)S(1)}, bf16[1,10,24,576]{3,2,0,1:T(8,128)(2,1)}, u32[]{:S(2)}) copy-start(bf16[1,10,24,576]{3,2,0,1:T(8,128)(2,1)} %stack.123) | copy-start | bytes 829444
  305.2 0.7 copy-start.23
  305.9 15.3 %copy-start = (f32[17,20,24,576]{3,2,1,0:T(8,128)}, f32[17,20,24,576]{3,2,1,0:T(8,128)S(1)}, u32[]{:S(2)}) copy-start(f32[17,20,24,576]{3,2,1,0:T(8,128)S(1)} %multiply_dynamic-update-slice_fusion) | copy-start | bytes 56401924
  305.9 15.3 %copy-start.17 = (f32[576,256,1,1]{1,0,3,2:T(8,128)S(1)}, f32[576,256,1,1]{1,0,3,2:T(8,128)}, u32[]{:S(2)}) copy-start(f32[576,256,1,1]{1,0,3,2:T(8,128)} %constant.259) | copy-start | bytes 1769476
  343.1 16.2 %copy-start.18 = (f32[256,16,1,1]{0,1,3,2:T(8,128)S(1)}, f32[256,16,1,1]{0,1,3,2:T(8,128)}, u32[]{:S(2)}) copy-start(f32[256,16,1,1]{0,1,3,2:T(8,128)} %constant.260) | copy-start | bytes 49156
  346.6 14.8 %copy-start.22 = (f32[16,24,1,1]{1,0,3,2:T(8,128)S(1)}, f32[16,24,1,1]{1,0,3,2:T(8,128)}, u32[]{:S(2)}) copy-start(f32[16,24,1,1]{1,0,3,2:T(8,128)} %constant.261) | copy-start | bytes 4612
  361.4 16.8 %copy-start.16 = (f32[576,256,1,1]{1,0,3,2:T(8,128)S(1)}, f32[576,256,1,1]{1,0,3,2:T(8,128)}, u32[]{:S(2)}) copy-start(f32[576,256,1,1]{1,0,3,2:T(8,128)} %constant.262) | copy-start | bytes 1769476
  401.6 14.8 %copy-start.21 = (f32[16,24,1,1]{1,0,3,2:T(8,128)S(1)}, f32[16,24,1,1]{1,0,3,2:T(8,128)}, u32[]{:S(2)}) copy-start(f32[16,24,1,1]{1,0,3,2:T(8,128)} %constant.263) | copy-start | bytes 4612
  416.4 16.7 %copy-start.15 = (f32[576,256,1,1]{1,0,3,2:T(8,128)S(1)}, f32[576,256,1,1]{1,0,3,2:T(8,128)}, u32[]{:S(2)}) copy-start(f32[576,256,1,1]{1,0,3,2:T(8,128)} %constant.264) | copy-start | bytes 1769476
  456.5 14.8 %copy-start.20 = (f32[16,24,1,1]{1,0,3,2:T(8,128)S(1)}, f32[16,24,1,1]{1,0,3,2:T(8,128)}, u32[]{:S(2)}) copy-start(f32[16,24,1,1]{1,0,3,2:T(8,128)} %constant.265) | copy-start | bytes 4612
  471.3 17.1 %copy-start.14 = (f32[576,256,1,1]{1,0,3,2:T(8,128)S(1)}, f32[576,256,1,1]{1,0,3,2:T(8,128)}, u32[]{:S(2)}) copy-start(f32[576,256,1,1]{1,0,3,2:T(8,128)} %constant.266) | copy-start | bytes 1769476
  515.4 11.5 %copy-start.24 = (pred[20]{0:T(512)(128)(4,1)S(1)}, pred[20]{0:T(512)(128)(4,1)}, u32[]{:S(2)}) copy-start(pred[20]{0:T(512)(128)(4,1)} %get-tuple-element.58) | copy-start | bytes 64
  524.4 50.6 %copy-start.26 = (f32[4,32]{1,0:T(4,128)S(1)}, f32[4,32]{1,0:T(4,128)}, u32[]{:S(2)}) copy-start(f32[4,32]{1,0:T(4,128)} %convolution_maximum_fusion) | copy-start | bytes 1540
  541.4 36.5 %all-to-all-start = ((f32[16,2,2048]{2,1,0:T(2,128)}), f32[16,2,2048]{2,1,0:T(2,128)}, u32[]{:S(2)}, u32[]{:S(2)}) async-start(f32[16,2,2048]{2,1,0:T(2,128)} %reshape.1064), calls=%async_computation | async-start | bytes 524288 | tf_op jit(solution)/shard_map/all_to_all | solution.py:173
